TPU v7x, 32 devices: a whole 2x2x4 slice. The times are simulated.
32 devices in a mesh: shard: 4 (over z), rep: 8 (over y, x, core).
Axes of the slice: x: 2, y: 2, z: 4, core: 2. Of those that a mesh axis runs over, the one named last changes fastest.
Arguments:
- grads: bfloat16 [1, 8192, 28672], P(None, 'shard', 'rep'), may hold values from -81 to 81
- seeds: int32 [1], replicated, may hold values from 0 to 999999
Outputs:
- projected: bfloat16 [512, 1, 28672], P('shard', None, 'rep')
All inputs are finite; a program needn't handle non-finite values.
Results may differ from a plain program's by a relative error of at most 0.0056.
Values may be sent and summed in bfloat16 or wider, within the bound.
No kernel may reach another device: no remote copies, remote signals or barrier semaphores. Data moves between devices by JAX's collectives and lax.ppermute only.
A program may use at most 128 MiB of HBM per device.

v0:
```python
import jax
import jax.numpy as jnp
from jax import lax
from jax.sharding import PartitionSpec as P

RANK = 512


mix_first = 668265263
mix_second = -2048144789
mix_third = -1028477387


def sketch_table(seeds, first_row, count, rank):
    rows = first_row + lax.iota(jnp.int32, count)
    columns = lax.iota(jnp.int32, rank)
    counter = rows[:, None] * jnp.int32(rank) + columns[None, :]
    hashed = jnp.bitwise_xor(counter[None, :, :], (seeds * jnp.int32(mix_first))[:, None, None])
    hashed = hashed * jnp.int32(mix_second)
    hashed = jnp.bitwise_xor(hashed, lax.shift_right_logical(hashed, jnp.int32(15)))
    hashed = hashed * jnp.int32(mix_third)
    hashed = jnp.bitwise_xor(hashed, lax.shift_right_logical(hashed, jnp.int32(13)))
    unit = lax.shift_right_logical(hashed, jnp.int32(8)).astype(jnp.float32) * (1.0 / 16777216.0)
    return (2.0 * unit - 1.0).astype(jnp.bfloat16)


def body(grads, seeds):
    mats, depth, width = grads.shape
    rows_whole = lax.all_to_all(grads, "rep", split_axis=1, concat_axis=2, tiled=True)
    block = rows_whole.shape[2] // 8

    def add_block(step, total):
        start = step * block
        table = sketch_table(seeds, start, block, RANK)
        piece = lax.dynamic_slice_in_dim(rows_whole, start, block, 2)
        return total + jnp.einsum("mdc,mcr->dmr", piece, table, preferred_element_type=jnp.float32)

    sketch_rows = lax.fori_loop(
        0, 8, add_block, jnp.zeros((rows_whole.shape[1], mats, RANK), jnp.float32)
    )
    local_gram = jnp.einsum(
        "dmr,dms->mrs",
        sketch_rows,
        sketch_rows,
        precision=lax.Precision.HIGHEST,
        preferred_element_type=jnp.float32,
    )
    gram = lax.psum(local_gram, ("shard", "rep"))
    factor = jnp.linalg.cholesky(gram)
    own_rows = jnp.transpose(sketch_rows, (1, 0, 2))
    basis_rows = lax.linalg.triangular_solve(
        factor, own_rows, left_side=False, lower=True, transpose_a=True
    ).astype(jnp.bfloat16)
    partial_sum = jnp.einsum(
        "mdr,mdc->rmc",
        lax.all_gather(basis_rows, "rep", axis=1, tiled=True),
        grads,
        preferred_element_type=jnp.float32,
    )
    projected = lax.psum_scatter(partial_sum, "shard", scatter_dimension=0, tiled=True)
    return projected.astype(jnp.bfloat16)


def solution(mesh):
    return jax.shard_map(
        body,
        mesh=mesh,
        in_specs=(P(None, "shard", "rep"), P()),
        out_specs=P("shard", None, "rep"),
        check_vma=False,
    )
```

profile of v0, /device:TPU:0, one launch (start us, length us, event | category | flops | bytes accessed | tf_op | source)
XLA Modules:
  0.0 861.7 jit_solution(14677463218900408071)
XLA Ops:
  6.5 26.0 %copy.30 = bf16[1,2048,3584]{2,0,1:T(2,128)(2,1)} copy(bf16[1,2048,3584]{2,1,0:T(8,128)(2,1)} %param.4) | data formatting | bytes 29360128 | tf_op args[0]
  33.1 94.1 %reduce.36 = bf16[2048,3584]{1,0:T(8,128)(2,1)} reduce(bf16[2048,1,3584]{2,1,0:T(2,128)(2,1)} %bitcast.210, bf16[]{:T(256)} %broadcast.502), dimensions={1}, to_apply=%bitcast.195.reduce_sub_computation | reduce | bytes 29360130
  127.2 16.3 %reshape.459 = bf16[8,2,458752]{2,1,0:T(2,128)(2,1)} reshape(bf16[2048,3584]{1,0:T(8,128)(2,1)} %reduce.36) | data formatting | bytes 29360128
  143.5 5.6 all-to-all-start
  150.2 161.0 %all-to-all-done = bf16[8,2,458752]{2,1,0:T(2,128)(2,1)} async-done(((bf16[8,2,458752]{2,1,0:T(2,128)(2,1)}), bf16[8,2,458752]{2,1,0:T(2,128)(2,1)}, u32[]{:S(2)}, u32[]{:S(2)}) %all-to-all-start) | async-done | bytes 14680096 | tf_op jit(solution)/shard_map/all_to_all | solution.py:29
  311.2 20.2 %reshape.460 = bf16[2048,1,3584]{2,1,0:T(2,128)(2,1)} reshape(bf16[8,2,458752]{2,1,0:T(2,128)(2,1)} %all-to-all-done) | data formatting | bytes 29360128
  331.4 19.4 %copy.28 = bf16[1,2048,3584]{2,1,0:T(8,128)(2,1)} copy(bf16[1,2048,3584]{2,0,1:T(2,128)(2,1)} %bitcast.211) | data formatting | bytes 29360128
  350.8 18.7 %copy.21 = bf16[1,256,8,3584]{1,3,2,0:T(8,128)(2,1)} copy(bf16[1,256,8,3584]{3,1,2,0:T(8,128)(2,1)} %bitcast.212) | data formatting | bytes 29360128 | tf_op jit(solution)/shard_map/all_to_all | solution.py:29
  369.5 42.8 %while.18 = (s32[]{:T(128)}, f32[256,1,512]{0,2,1:T(8,128)S(1)}, s32[1]{0:T(128)}, bf16[1,256,28672]{1,2,0:T(8,128)(2,1)}, s32[]{:T(128)}, /*index=5*/s32[]{:T(128)}, s32[]{:T(128)}, s32[]{:T(128)}) while((s32[]{:T(128)}, f32[256,1,512]{0,2,1:T(8,128)S(1)}, s32[1]{0:T(128)}, bf16[1,256,28672]{1,2,0:T(8,128)(2,1)}, s32[]{:T(128)}, ...), condition=%wide.region_1.0_spmd.clone, body=%wide.region_0.0_spmd.clone.sunk | while | flops 963648512 | bytes 2912917 | solution.py:38
  369.5 5.3 fusion.77
  374.8 5.3 fusion.77
  380.2 5.3 fusion.77
  385.5 5.3 fusion.77
  390.9 5.3 fusion.77
  396.2 5.3 fusion.77
  401.6 5.3 fusion.77
  407.0 5.3 fusion.77
  412.3 2.1 convolution_bitcast_fusion
  414.8 130.7 %all-reduce.3.cloned.1.call-done = f32[1,512,512]{1,2,0:T(8,128)} async-done(((f32[1,512,512]{1,2,0:T(8,128)}), f32[1,512,512]{1,2,0:T(8,128)}) %all-reduce.3.cloned.1.call-update) | async-done | bytes 1048592 | tf_op jit(solution)/shard_map/psum | solution.py:48
  545.5 1.6 copy.25
  547.1 1.4 fusion.47
  548.5 11.7 %custom-call.34 = f32[1,128,128]{2,1,0:T(8,128)S(1)} custom-call(f32[1,128,128]{2,1,0:T(8,128)S(1)} %cholesky.267), custom_call_target="Cholesky" | custom-call | tf_op jit(solution)/shard_map/jit(cholesky)/cholesky | solution.py:49
  560.3 9.8 %custom-call.35 = f32[1,1,128,128]{2,3,1,0:T(8,128)S(1)} custom-call(f32[1,1,128,128]{3,2,1,0:T(8,128)S(1)} %get-tuple-element.173), custom_call_target="InvertDiagBlocksLowerTriangular" | custom-call | tf_op jit(solution)/shard_map/jit(cholesky)/cholesky | solution.py:49
  570.9 11.7 %custom-call.36 = f32[1,128,128]{2,1,0:T(8,128)S(1)} custom-call(f32[1,128,128]{2,1,0:T(8,128)S(1)} %cholesky.271), custom_call_target="Cholesky" | custom-call | tf_op jit(solution)/shard_map/jit(cholesky)/cholesky | solution.py:49
  582.7 10.0 %custom-call.37 = f32[1,1,128,128]{2,3,1,0:T(8,128)S(1)} custom-call(f32[1,1,128,128]{3,2,1,0:T(8,128)S(1)} %get-tuple-element.170), custom_call_target="InvertDiagBlocksLowerTriangular" | custom-call | tf_op jit(solution)/shard_map/jit(cholesky)/cholesky | solution.py:49
  593.3 11.7 %custom-call.38 = f32[1,128,128]{2,1,0:T(8,128)S(1)} custom-call(f32[1,128,128]{2,1,0:T(8,128)S(1)} %cholesky.276), custom_call_target="Cholesky" | custom-call | tf_op jit(solution)/shard_map/jit(cholesky)/cholesky | solution.py:49
  605.1 0.7 compare_reduce_fusion.1
  605.8 9.8 %custom-call.39 = f32[1,1,128,128]{2,3,1,0:T(8,128)S(1)} custom-call(f32[1,1,128,128]{3,2,1,0:T(8,128)S(1)} %get-tuple-element.167), custom_call_target="InvertDiagBlocksLowerTriangular" | custom-call | tf_op jit(solution)/shard_map/jit(cholesky)/cholesky | solution.py:49
  616.2 11.7 %custom-call.40 = f32[1,128,128]{2,1,0:T(8,128)S(1)} custom-call(f32[1,128,128]{2,1,0:T(8,128)S(1)} %fusion.46), custom_call_target="Cholesky" | custom-call | tf_op jit(solution)/shard_map/jit(cholesky)/cholesky | solution.py:49
  628.0 0.6 compare_reduce_fusion
  628.6 0.9 compare_reduce_fusion.2
  632.2 8.1 while.17
  632.3 0.6 fusion.74
  632.9 1.3 bitcast_dynamic-update-slice_fusion.2
  634.3 0.6 fusion.74
  634.9 1.3 bitcast_dynamic-update-slice_fusion.2
  636.4 0.6 fusion.74
  637.0 1.3 bitcast_dynamic-update-slice_fusion.2
  638.4 0.6 fusion.74
  639.0 1.3 bitcast_dynamic-update-slice_fusion.2
  640.4 39.3 %custom-call.41 = f32[1,4,128,128]{2,3,1,0:T(8,128)S(1)} custom-call(f32[1,4,128,128]{3,2,1,0:T(8,128)S(1)} %bitcast.221), custom_call_target="InvertDiagBlocksLowerTriangular" | custom-call | tf_op jit(solution)/shard_map/triangular_solve | solution.py:51
  680.7 0.6 fusion.41
  681.7 0.8 fusion.43
  682.8 0.7 pad_maximum_fusion
  683.6 27.2 %all-gather.2.cloned.1.call-done = bf16[1,2048,512]{1,2,0:T(8,128)(2,1)} async-done(((bf16[1,256,512]{1,2,0:T(8,128)(2,1)}), bf16[1,2048,512]{1,2,0:T(8,128)(2,1)}) %all-gather.2.cloned.1.call-update) | async-done | bytes 2097168 | tf_op jit(solution)/shard_map/all_gather | solution.py:56
  710.8 13.5 %fusion.31 = f32[512,1,3584]{2,0,1:T(8,128)} fusion(bf16[1,2048,3584]{2,1,0:T(8,128)(2,1)} %param.4, bf16[1,2048,512]{1,2,0:T(8,128)(2,1)} %all-gather.2.cloned.1.call-done), kind=kOutput, calls=%fused_computation.27 | convolution fusion | flops 7516192768 | bytes 24117248 | tf_op jit(solution)/shard_map/mdr,mdc->rmc/dot_general | solution.py:54
  724.3 127.9 %reduce-scatter.2.cloned.1.call-done = f32[128,1,3584]{2,0,1:T(8,128)} async-done(((f32[512,1,3584]{2,0,1:T(8,128)}), f32[128,1,3584]{2,0,1:T(8,128)}) %reduce-scatter.2.cloned.1.call-update) | async-done | bytes 1835024 | tf_op jit(solution)/shard_map/reduce_scatter | solution.py:60
  852.3 2.5 convert_element_type.66
  (44 shorter events, 5.8 us)
Async XLA Ops:
  143.5 167.7 %all-to-all-start = ((bf16[8,2,458752]{2,1,0:T(2,128)(2,1)}), bf16[8,2,458752]{2,1,0:T(2,128)(2,1)}, u32[]{:S(2)}, u32[]{:S(2)}) async-start(bf16[8,2,458752]{2,1,0:T(2,128)(2,1)} %reshape.459), calls=%async_computation | async-start | bytes 29360128 | tf_op jit(solution)/shard_map/all_to_all | solution.py:29
  149.1 396.5 %all-reduce.3.cloned.1.call-start = ((), (), s32[]{:S(2)}) async-start(), calls=%async_computation.2 | async-start | bytes 2097152 | tf_op jit(solution)/shard_map/psum | solution.py:48
  414.4 296.4 %all-gather.2.cloned.1.call-start = ((), (), s32[]{:S(2)}) async-start(), calls=%async_computation.3 | async-start | bytes 2359296 | tf_op jit(solution)/shard_map/all_gather | solution.py:56
  683.6 168.7 %reduce-scatter.2.cloned.1.call-start = ((), (), s32[]{:S(2)}) async-start(), calls=%async_computation.4 | async-start | bytes 9175040 | tf_op jit(solution)/shard_map/reduce_scatter | solution.py:60
Sparse Core Ops, SparseCore 0:
  414.5 130.9 all-reduce.2
  683.7 27.0 all-gather.1
  724.5 127.7 reduce-scatter.1
where the time goes:
time: 869 us; the launch traced here: 862 us
  waiting for transfers between devices  447 us (51%)
  other arithmetic  217 us (25%)
  local copies, waits for them, and re-layouts  111 us (13%)
  matrix products  63 us (7%)
  between operations  17 us (2%)
    all_to_all x1, waiting for transfers between devices, body(): lax.all_to_all(grads, 'rep', split_axis=1, concat_axis=2, tiled=True)  161 us
    psum x1, waiting for transfers between devices, body(): gram = lax.psum(local_gram, ('shard', 'rep'))  131 us
    reduce_scatter x1, waiting for transfers between devices, body(): lax.psum_scatter(partial_sum, 'shard', scatter_dimension=0, tiled=True)  128 us
    unnamed x3, other arithmetic  94.1 us
    unnamed x5, local copies, waits for them, and re-layouts  82.4 us
    another operation x14, other arithmetic, body(): factor = jnp.linalg.cholesky(gram)  78.9 us
    dot_general x8, matrix products, add_block(): jnp.einsum('mdc,mcr->dmr', piece, table, preferred_element_type=jnp.float32)  42.5 us
    another operation x4, other arithmetic, body(): lax.linalg.triangular_solve(factor, own_rows, left_side=False, lower=True...  40.2 us
  transfers between devices with their start and end apart: 4, of which 4 were waited for; matrix products, arithmetic and copies ran while one was open for 0% of the time, Pallas kernels for 0%

commit v1 on v0

v1 whole, which is shorter than its diff:
```python
import jax
import jax.numpy as jnp
from jax import lax
from jax.sharding import PartitionSpec as P

RANK = 512


mix_first = 668265263
mix_second = -2048144789
mix_third = -1028477387


def sketch_table(seeds, first_row, count, rank):
    rows = first_row + lax.iota(jnp.int32, count)
    columns = lax.iota(jnp.int32, rank)
    counter = rows[:, None] * jnp.int32(rank) + columns[None, :]
    hashed = jnp.bitwise_xor(counter[None, :, :], (seeds * jnp.int32(mix_first))[:, None, None])
    hashed = hashed * jnp.int32(mix_second)
    hashed = jnp.bitwise_xor(hashed, lax.shift_right_logical(hashed, jnp.int32(15)))
    hashed = hashed * jnp.int32(mix_third)
    hashed = jnp.bitwise_xor(hashed, lax.shift_right_logical(hashed, jnp.int32(13)))
    unit = lax.shift_right_logical(hashed, jnp.int32(8)).astype(jnp.float32) * (1.0 / 16777216.0)
    return (2.0 * unit - 1.0).astype(jnp.bfloat16)


def body(grads, seeds):
    mats, depth, width = grads.shape
    col0 = lax.axis_index("rep") * width
    outs = []
    for m in range(mats):
        table = sketch_table(seeds[m:m + 1], col0, width, RANK)[0]
        g = grads[m]
        partial = jnp.dot(g, table, preferred_element_type=jnp.float32)
        sketch_rows = lax.psum(partial, "rep")
        local_gram = jnp.dot(
            sketch_rows.T, sketch_rows,
            precision=lax.Precision.HIGHEST,
            preferred_element_type=jnp.float32,
        )
        gram = lax.psum(local_gram, "shard")
        factor = jnp.linalg.cholesky(gram)
        basis_rows = lax.linalg.triangular_solve(
            factor, sketch_rows, left_side=False, lower=True, transpose_a=True
        ).astype(jnp.bfloat16)
        partial_sum = jnp.dot(basis_rows.T, g, preferred_element_type=jnp.float32)
        outs.append(partial_sum)
    partial_sum = jnp.stack(outs, axis=1)
    projected = lax.psum_scatter(partial_sum, "shard", scatter_dimension=0, tiled=True)
    return projected.astype(jnp.bfloat16)


def solution(mesh):
    return jax.shard_map(
        body,
        mesh=mesh,
        in_specs=(P(None, "shard", "rep"), P()),
        out_specs=P("shard", None, "rep"),
        check_vma=False,
    )
```

time: 869 us -> 481 us (0.55)
  waiting for transfers between devices: 447 us -> 263 us
  local copies, waits for them, and re-layouts: 111 us -> 9.44 us
  other arithmetic: 217 us -> 131 us
  matrix products: 63 us -> 53.5 us
    all_to_all x1 -> x0, waiting for transfers between devices: 161 us -> none  [body(): lax.all_to_all(grads, 'rep', split_axis=1, concat_axis=2, tiled=True)]
    unnamed x3 -> x1, other arithmetic: 94.1 us -> 0.01 us
    unnamed x5 -> x2, local copies, waits for them, and re-layouts: 82.4 us -> 0.01 us
    all_gather x1 -> x0, waiting for transfers between devices: 27.2 us -> none  [body(): lax.all_gather(basis_rows, 'rep', axis=1, tiled=True)]
    all_to_all x1 -> x0, local copies, waits for them, and re-layouts: 18.7 us -> none  [body(): lax.all_to_all(grads, 'rep', split_axis=1, concat_axis=2, tiled=True)]
    dot_general x10 -> x3, matrix products: 58.1 us -> 40.1 us  [the longest x1 16.7 us: body(): partial = jnp.dot(g, table, preferred_element_type=jnp.float32)]
    psum x1 -> x2, waiting for transfers between devices: 131 us -> 135 us  [the longest x1 83.4 us: body(): sketch_rows = lax.psum(partial, 'rep')]
    another operation x4 -> x3, other arithmetic: 40.2 us -> 39.7 us  [body(): lax.linalg.triangular_solve(factor, sketch_rows, left_side=False, lower=T...]
  transfers between devices with their start and end apart: 4 -> 3, of which waited for: 4 -> 3; matrix products, arithmetic and copies ran while one was open for 0% -> 0% of each run, Pallas kernels for 0% -> 0%
where the time goes in v1:
time: 481 us; the launch traced here: 474 us
  waiting for transfers between devices  263 us (55%)
  other arithmetic  131 us (27%)
  matrix products  53.5 us (11%)
  between operations  16.9 us (4%)
  local copies, waits for them, and re-layouts  9.44 us (2%)
    reduce_scatter x1, waiting for transfers between devices, body(): lax.psum_scatter(partial_sum, 'shard', scatter_dimension=0, tiled=True)  127 us
    another operation x14, other arithmetic, body(): factor = jnp.linalg.cholesky(gram)  87.2 us
    psum x1, waiting for transfers between devices, body(): sketch_rows = lax.psum(partial, 'rep')  83.4 us
    psum x1, waiting for transfers between devices, body(): gram = lax.psum(local_gram, 'shard')  52 us
    another operation x3, other arithmetic, body(): lax.linalg.triangular_solve(factor, sketch_rows, left_side=False, lower=T...  39.7 us
    dot_general x1, matrix products, body(): partial = jnp.dot(g, table, preferred_element_type=jnp.float32)  16.7 us
    dot_general x1, matrix products, body(): partial_sum = jnp.dot(basis_rows.T, g, preferred_element_type=jnp.float32)  13.1 us
    another operation x7, matrix products, body(): lax.linalg.triangular_solve(factor, sketch_rows, left_side=False, lower=T...  11.5 us
  transfers between devices with their start and end apart: 3, of which 3 were waited for; matrix products, arithmetic and copies ran while one was open for 0% of the time, Pallas kernels for 0%

profile of v1, /device:TPU:0, one launch (start us, length us, event | category | flops | bytes accessed | tf_op | source)
XLA Modules:
  0.0 473.7 jit_solution(5773051382835369046)
XLA Ops:
  7.2 16.7 %fusion.24 = f32[2048,512]{0,1:T(8,128)} fusion(bf16[1,2048,3584]{2,1,0:T(8,128)(2,1)} %param.2, s32[]{:T(128)} %bitcast, s32[3584]{0:T(1024)S(1)} %add_multiply_fusion), kind=kOutput, calls=%fused_computation.25 | convolution fusion | flops 7540047872 | bytes 18888708 | tf_op jit(solution)/shard_map/dot_general | solution.py:34
  23.9 0.3 all-reduce.6.cloned.1.call-start
  24.3 83.4 %all-reduce.4.cloned.1.call-done = f32[2048,512]{0,1:T(8,128)} async-done(((f32[2048,512]{0,1:T(8,128)}), f32[2048,512]{0,1:T(8,128)}) %all-reduce.4.cloned.1.call-update) | async-done | bytes 4194320 | tf_op jit(solution)/shard_map/psum | solution.py:35
  107.6 10.2 %fusion.81 = f32[512,512]{0,1:T(8,128)} fusion(f32[2048,512]{0,1:T(8,128)} %all-reduce.4.cloned.1.call-done), kind=kOutput, calls=%fused_computation.110 | convolution fusion | flops 6442450944 | bytes 5242880 | tf_op jit(solution)/shard_map/dot_general | solution.py:36
  118.0 52.0 %all-reduce.6.cloned.1.call-done = f32[512,512]{0,1:T(8,128)} async-done(((f32[512,512]{0,1:T(8,128)}), f32[512,512]{0,1:T(8,128)}) %all-reduce.6.cloned.1.call-update) | async-done | bytes 1048592 | tf_op jit(solution)/shard_map/psum | solution.py:41
  170.0 1.6 copy.6
  171.6 1.4 fusion.50
  173.0 11.7 %cholesky.104 = f32[128,128]{1,0:T(8,128)S(1)} custom-call(f32[128,128]{1,0:T(8,128)S(1)} %cholesky.266), custom_call_target="Cholesky" | custom-call | tf_op jit(solution)/shard_map/jit(cholesky)/cholesky | solution.py:42
  184.8 9.8 %custom-call.30 = f32[1,128,128]{1,2,0:T(8,128)S(1)} custom-call(f32[1,128,128]{2,1,0:T(8,128)S(1)} %get-tuple-element.32), custom_call_target="InvertDiagBlocksLowerTriangular" | custom-call | tf_op jit(solution)/shard_map/jit(cholesky)/cholesky | solution.py:42
  194.6 0.1 cholesky.224
  194.7 0.3 constant_dynamic-update-slice_fusion.3
  195.1 0.3 convolution_subtract_fusion.2
  195.4 11.7 %cholesky.217 = f32[128,128]{1,0:T(8,128)S(1)} custom-call(f32[128,128]{1,0:T(8,128)S(1)} %cholesky.270), custom_call_target="Cholesky" | custom-call | tf_op jit(solution)/shard_map/jit(cholesky)/cholesky | solution.py:42
  207.2 18.5 %custom-call.31 = f32[1,128,128]{1,2,0:T(8,128)S(1)} custom-call(f32[1,128,128]{2,1,0:T(8,128)S(1)} %get-tuple-element.29), custom_call_target="InvertDiagBlocksLowerTriangular" | custom-call | tf_op jit(solution)/shard_map/jit(cholesky)/cholesky | solution.py:42
  225.7 0.3 convolution_dynamic-update-slice_fusion
  225.9 0.4 convolution_subtract_fusion.3
  226.3 11.7 %cholesky.238 = f32[128,128]{1,0:T(8,128)S(1)} custom-call(f32[128,128]{1,0:T(8,128)S(1)} %cholesky.275), custom_call_target="Cholesky" | custom-call | tf_op jit(solution)/shard_map/jit(cholesky)/cholesky | solution.py:42
  238.1 0.7 compare_reduce_fusion.1
  238.7 9.8 %custom-call.32 = f32[1,128,128]{1,2,0:T(8,128)S(1)} custom-call(f32[1,128,128]{2,1,0:T(8,128)S(1)} %get-tuple-element.26), custom_call_target="InvertDiagBlocksLowerTriangular" | custom-call | tf_op jit(solution)/shard_map/jit(cholesky)/cholesky | solution.py:42
  248.6 0.2 convolution_dynamic-update-slice_fusion.1
  248.8 0.4 convolution_subtract_fusion.4
  249.2 11.7 %cholesky.255 = f32[128,128]{1,0:T(8,128)S(1)} custom-call(f32[128,128]{1,0:T(8,128)S(1)} %convolution_subtract_fusion.4), custom_call_target="Cholesky" | custom-call | tf_op jit(solution)/shard_map/jit(cholesky)/cholesky | solution.py:42
  260.9 0.7 compare_reduce_fusion
  261.6 0.7 compare_reduce_fusion.2
  264.8 0.3 select_select_fusion
  265.1 7.8 %while.1 = (s32[]{:T(128)}, f32[512,512]{1,0:T(8,128)S(1)}, s32[4,2]{0,1:T(2,128)S(1)}, f32[4,128,128]{2,1,0:T(8,128)S(1)}, s32[]{:T(128)}) while((s32[]{:T(128)}, f32[512,512]{1,0:T(8,128)S(1)}, s32[4,2]{0,1:T(2,128)S(1)}, f32[4,128,128]{2,1,0:T(8,128)S(1)}, s32[]{:T(128)}) %tuple.30), condition=%wide.while_cond, body=%wide.while_body.sunk | while | flops 2 | bytes 131189 | solution.py:43
  265.2 0.1 constant_dynamic-slice_fusion.2
  265.2 0.5 fusion.90
  265.8 1.3 bitcast_dynamic-update-slice_fusion.2
  267.1 0.1 constant_dynamic-slice_fusion.2
  267.2 0.5 fusion.90
  267.7 1.3 bitcast_dynamic-update-slice_fusion.2
  269.1 0.1 constant_dynamic-slice_fusion.2
  269.1 0.5 fusion.90
  269.7 1.3 bitcast_dynamic-update-slice_fusion.2
  271.1 0.5 fusion.90
  271.6 1.3 bitcast_dynamic-update-slice_fusion.2
  273.0 39.3 %custom-call.33 = f32[4,128,128]{1,2,0:T(8,128)S(1)} custom-call(f32[4,128,128]{2,1,0:T(8,128)S(1)} %get-tuple-element.12), custom_call_target="InvertDiagBlocksLowerTriangular" | custom-call | tf_op jit(solution)/shard_map/triangular_solve | solution.py:43
  312.3 2.5 fusion.80
  314.8 2.3 convolution_subtract_fusion.1
  317.1 1.1 fusion.79
  318.2 1.3 convolution_subtract_fusion
  319.5 1.1 fusion.78
  320.6 2.2 fusion.35
  322.8 1.1 convolution_convert_fusion
  323.9 13.1 %fusion.10 = f32[512,1,3584]{2,0,1:T(8,128)} fusion(bf16[1,2048,3584]{2,1,0:T(8,128)(2,1)} %param.2, bf16[2048,128]{0,1:T(8,128)(2,1)S(1)} %convolution_convert_fusion, bf16[2048,128]{0,1:T(8,128)(2,1)S(1)} %get-tuple-element.35, bf16[2048,128]{0,1:T(8,128)(2,1)S(1)} %get-tuple-element.37, bf16[2048,128]{0,1:T(8,128)(2,1)S(1)} %get-tuple-element.39), kind=kOutput, calls=%fused_computation.14 | convolution fusion | flops 7524581376 | bytes 24117248 | tf_op jit(solution)/shard_map/dot_general | solution.py:46
  337.0 127.2 %reduce-scatter.2.cloned.1.call-done = f32[128,1,3584]{2,0,1:T(8,128)} async-done(((f32[512,1,3584]{2,0,1:T(8,128)}), f32[128,1,3584]{2,0,1:T(8,128)}) %reduce-scatter.2.cloned.1.call-update) | async-done | bytes 1835024 | tf_op jit(solution)/shard_map/reduce_scatter | solution.py:49
  464.2 2.5 convert_element_type.47
  (19 shorter events, 0.4 us)
Async XLA Ops:
  6.5 101.1 %all-reduce.4.cloned.1.call-start = ((), (), s32[]{:S(2)}) async-start(), calls=%async_computation.1 | async-start | bytes 8388608 | tf_op jit(solution)/shard_map/psum | solution.py:35
  23.9 146.1 %all-reduce.6.cloned.1.call-start = ((), (), s32[]{:S(2)}) async-start(), calls=%async_computation.2 | async-start | bytes 2097152 | tf_op jit(solution)/shard_map/psum | solution.py:41
  117.9 346.3 %reduce-scatter.2.cloned.1.call-start = ((), (), s32[]{:S(2)}) async-start(), calls=%async_computation.3 | async-start | bytes 9175040 | tf_op jit(solution)/shard_map/reduce_scatter | solution.py:49
  312.3 5.9 %copy-start = (f32[2048,512]{0,1:T(8,128)S(1)}, f32[2048,512]{0,1:T(8,128)}, u32[]{:S(2)}) copy-start(f32[2048,512]{0,1:T(8,128)} %all-reduce.4.cloned.1.call-done) | copy-start | bytes 12582916
Sparse Core Ops, SparseCore 0:
  24.1 83.5 all-reduce.3
  118.0 51.9 all-reduce.5
  337.1 127.0 reduce-scatter.1

commit v2 on v1

--- a/solution.py
+++ b/solution.py
@@ -38,7 +38,11 @@
             precision=lax.Precision.HIGHEST,
             preferred_element_type=jnp.float32,
         )
-        gram = lax.psum(local_gram, "shard")
+        piece = local_gram.shape[0] // lax.axis_size("rep")
+        mine = lax.dynamic_slice_in_dim(
+            local_gram, lax.axis_index("rep") * piece, piece, 0
+        )
+        gram = lax.all_gather(lax.psum(mine, "shard"), "rep", axis=0, tiled=True)
         factor = jnp.linalg.cholesky(gram)
         basis_rows = lax.linalg.triangular_solve(
             factor, sketch_rows, left_side=False, lower=True, transpose_a=True

time: 481 us -> 490 us (1.019)
  waiting for transfers between devices: 263 us -> 271 us
    all_gather x0 -> x1, waiting for transfers between devices: none -> 24.9 us  [body(): gram = lax.all_gather(lax.psum(mine, 'shard'), 'rep', axis=0, tiled=True)]
    psum x1, waiting for transfers between devices: 52 us -> 34.8 us  [body(): gram = lax.all_gather(lax.psum(mine, 'shard'), 'rep', axis=0, tiled=True)]
  transfers between devices with their start and end apart: 3 -> 4, of which waited for: 3 -> 4; matrix products, arithmetic and copies ran while one was open for 0% -> 0% of each run, Pallas kernels for 0% -> 0%
where the time goes in v2:
time: 490 us; the launch traced here: 482 us
  waiting for transfers between devices  271 us (55%)
  other arithmetic  131 us (27%)
  matrix products  52.5 us (11%)
  between operations  17 us (3%)
  local copies, waits for them, and re-layouts  10.2 us (2%)
    reduce_scatter x1, waiting for transfers between devices, body(): lax.psum_scatter(partial_sum, 'shard', scatter_dimension=0, tiled=True)  128 us
    another operation x14, other arithmetic, body(): factor = jnp.linalg.cholesky(gram)  87.2 us
    psum x1, waiting for transfers between devices, body(): sketch_rows = lax.psum(partial, 'rep')  83.4 us
    another operation x3, other arithmetic, body(): lax.linalg.triangular_solve(factor, sketch_rows, left_side=False, lower=T...  39.7 us
    psum x1, waiting for transfers between devices, body(): gram = lax.all_gather(lax.psum(mine, 'shard'), 'rep', axis=0, tiled=True)  34.8 us
    all_gather x1, waiting for transfers between devices, body(): gram = lax.all_gather(lax.psum(mine, 'shard'), 'rep', axis=0, tiled=True)  24.9 us
    dot_general x1, matrix products, body(): partial = jnp.dot(g, table, preferred_element_type=jnp.float32)  16.7 us
    dot_general x1, matrix products, body(): partial_sum = jnp.dot(basis_rows.T, g, preferred_element_type=jnp.float32)  13.1 us
  transfers between devices with their start and end apart: 4, of which 4 were waited for; matrix products, arithmetic and copies ran while one was open for 0% of the time, Pallas kernels for 0%

profile of v2, /device:TPU:0, one launch (start us, length us, event | category | flops | bytes accessed | tf_op | source)
XLA Modules:
  0.0 482.1 jit_solution(17405715005233900256)
XLA Ops:
  7.2 16.7 %fusion.24 = f32[2048,512]{0,1:T(8,128)} fusion(bf16[1,2048,3584]{2,1,0:T(8,128)(2,1)} %param.2, s32[]{:T(128)} %bitcast, s32[3584]{0:T(1024)S(1)} %add_multiply_fusion), kind=kOutput, calls=%fused_computation.25 | convolution fusion | flops 7540047872 | bytes 18888708 | tf_op jit(solution)/shard_map/dot_general | solution.py:34
  23.9 0.3 all-reduce.6.cloned.1.call-start
  24.3 83.4 %all-reduce.4.cloned.1.call-done = f32[2048,512]{0,1:T(8,128)} async-done(((f32[2048,512]{0,1:T(8,128)}), f32[2048,512]{0,1:T(8,128)}) %all-reduce.4.cloned.1.call-update) | async-done | bytes 4194320 | tf_op jit(solution)/shard_map/psum | solution.py:35
  107.6 9.3 %fusion.81 = f32[512,512]{1,0:T(8,128)S(1)} fusion(f32[2048,512]{0,1:T(8,128)} %all-reduce.4.cloned.1.call-done), kind=kOutput, calls=%fused_computation.111 | convolution fusion | flops 6442450944 | bytes 5242880 | tf_op jit(solution)/shard_map/dot_general | solution.py:36
  117.0 0.7 constant_dynamic-slice_fusion.1
  117.7 34.8 %all-reduce.6.cloned.1.call-done = f32[64,512]{1,0:T(8,128)} async-done(((f32[64,512]{1,0:T(8,128)}), f32[64,512]{1,0:T(8,128)}) %all-reduce.6.cloned.1.call-update) | async-done | bytes 131088 | tf_op jit(solution)/shard_map/psum | solution.py:45
  152.6 24.9 %all-gather.2.cloned.1.call-done = f32[512,512]{1,0:T(8,128)} async-done(((f32[64,512]{1,0:T(8,128)}), f32[512,512]{1,0:T(8,128)}) %all-gather.2.cloned.1.call-update) | async-done | bytes 1048592 | tf_op jit(solution)/shard_map/all_gather | solution.py:45
  177.5 1.6 copy.7
  179.1 1.4 fusion.50
  180.6 11.7 %cholesky.104 = f32[128,128]{1,0:T(8,128)S(1)} custom-call(f32[128,128]{1,0:T(8,128)S(1)} %cholesky.266), custom_call_target="Cholesky" | custom-call | tf_op jit(solution)/shard_map/jit(cholesky)/cholesky | solution.py:46
  192.3 9.8 %custom-call.30 = f32[1,128,128]{1,2,0:T(8,128)S(1)} custom-call(f32[1,128,128]{2,1,0:T(8,128)S(1)} %get-tuple-element.32), custom_call_target="InvertDiagBlocksLowerTriangular" | custom-call | tf_op jit(solution)/shard_map/jit(cholesky)/cholesky | solution.py:46
  202.1 0.1 cholesky.224
  202.3 0.3 constant_dynamic-update-slice_fusion.3
  202.6 0.3 convolution_subtract_fusion.2
  202.9 11.7 %cholesky.217 = f32[128,128]{1,0:T(8,128)S(1)} custom-call(f32[128,128]{1,0:T(8,128)S(1)} %cholesky.270), custom_call_target="Cholesky" | custom-call | tf_op jit(solution)/shard_map/jit(cholesky)/cholesky | solution.py:46
  214.7 18.5 %custom-call.31 = f32[1,128,128]{1,2,0:T(8,128)S(1)} custom-call(f32[1,128,128]{2,1,0:T(8,128)S(1)} %get-tuple-element.29), custom_call_target="InvertDiagBlocksLowerTriangular" | custom-call | tf_op jit(solution)/shard_map/jit(cholesky)/cholesky | solution.py:46
  233.2 0.3 convolution_dynamic-update-slice_fusion
  233.5 0.4 convolution_subtract_fusion.3
  233.9 11.7 %cholesky.238 = f32[128,128]{1,0:T(8,128)S(1)} custom-call(f32[128,128]{1,0:T(8,128)S(1)} %cholesky.275), custom_call_target="Cholesky" | custom-call | tf_op jit(solution)/shard_map/jit(cholesky)/cholesky | solution.py:46
  245.6 0.7 compare_reduce_fusion.1
  246.3 9.8 %custom-call.32 = f32[1,128,128]{1,2,0:T(8,128)S(1)} custom-call(f32[1,128,128]{2,1,0:T(8,128)S(1)} %get-tuple-element.26), custom_call_target="InvertDiagBlocksLowerTriangular" | custom-call | tf_op jit(solution)/shard_map/jit(cholesky)/cholesky | solution.py:46
  256.1 0.2 convolution_dynamic-update-slice_fusion.1
  256.3 0.4 convolution_subtract_fusion.4
  256.7 11.7 %cholesky.255 = f32[128,128]{1,0:T(8,128)S(1)} custom-call(f32[128,128]{1,0:T(8,128)S(1)} %convolution_subtract_fusion.4), custom_call_target="Cholesky" | custom-call | tf_op jit(solution)/shard_map/jit(cholesky)/cholesky | solution.py:46
  268.4 0.7 compare_reduce_fusion
  269.1 0.7 compare_reduce_fusion.2
  272.4 0.3 select_select_fusion
  272.7 7.9 %while.1 = (s32[]{:T(128)}, f32[512,512]{1,0:T(8,128)S(1)}, s32[4,2]{0,1:T(2,128)S(1)}, f32[4,128,128]{2,1,0:T(8,128)S(1)}, s32[]{:T(128)}) while((s32[]{:T(128)}, f32[512,512]{1,0:T(8,128)S(1)}, s32[4,2]{0,1:T(2,128)S(1)}, f32[4,128,128]{2,1,0:T(8,128)S(1)}, s32[]{:T(128)}) %tuple.30), condition=%wide.while_cond, body=%wide.while_body.sunk | while | flops 2 | bytes 131189 | solution.py:47
  272.8 0.5 fusion.90
  273.4 1.4 bitcast_dynamic-update-slice_fusion.2
  274.7 0.1 constant_dynamic-slice_fusion.3
  274.8 0.5 fusion.90
  275.3 1.4 bitcast_dynamic-update-slice_fusion.2
  276.8 0.5 fusion.90
  277.3 1.4 bitcast_dynamic-update-slice_fusion.2
  278.8 0.5 fusion.90
  279.3 1.4 bitcast_dynamic-update-slice_fusion.2
  280.7 39.3 %custom-call.33 = f32[4,128,128]{1,2,0:T(8,128)S(1)} custom-call(f32[4,128,128]{2,1,0:T(8,128)S(1)} %get-tuple-element.12), custom_call_target="InvertDiagBlocksLowerTriangular" | custom-call | tf_op jit(solution)/shard_map/triangular_solve | solution.py:47
  320.0 2.5 fusion.80
  322.4 2.3 convolution_subtract_fusion.1
  324.8 1.1 fusion.79
  325.8 1.3 convolution_subtract_fusion
  327.2 1.1 fusion.78
  328.3 2.2 fusion.35
  330.5 1.1 convolution_convert_fusion
  331.6 13.1 %fusion.10 = f32[512,1,3584]{2,0,1:T(8,128)} fusion(bf16[1,2048,3584]{2,1,0:T(8,128)(2,1)} %param.2, bf16[2048,128]{0,1:T(8,128)(2,1)S(1)} %convolution_convert_fusion, bf16[2048,128]{0,1:T(8,128)(2,1)S(1)} %get-tuple-element.35, bf16[2048,128]{0,1:T(8,128)(2,1)S(1)} %get-tuple-element.37, bf16[2048,128]{0,1:T(8,128)(2,1)S(1)} %get-tuple-element.39), kind=kOutput, calls=%fused_computation.14 | convolution fusion | flops 7524581376 | bytes 24117248 | tf_op jit(solution)/shard_map/dot_general | solution.py:50
  344.7 127.9 %reduce-scatter.2.cloned.1.call-done = f32[128,1,3584]{2,0,1:T(8,128)} async-done(((f32[512,1,3584]{2,0,1:T(8,128)}), f32[128,1,3584]{2,0,1:T(8,128)}) %reduce-scatter.2.cloned.1.call-update) | async-done | bytes 1835024 | tf_op jit(solution)/shard_map/reduce_scatter | solution.py:53
  472.6 2.5 convert_element_type.47
  (23 shorter events, 0.6 us)
Async XLA Ops:
  6.5 101.1 %all-reduce.4.cloned.1.call-start = ((), (), s32[]{:S(2)}) async-start(), calls=%async_computation.1 | async-start | bytes 8388608 | tf_op jit(solution)/shard_map/psum | solution.py:35
  23.9 128.6 %all-reduce.6.cloned.1.call-start = ((), (), s32[]{:S(2)}) async-start(), calls=%async_computation.2 | async-start | bytes 262144 | tf_op jit(solution)/shard_map/psum | solution.py:45
  117.7 59.9 %all-gather.2.cloned.1.call-start = ((), (), s32[]{:S(2)}) async-start(), calls=%async_computation.3 | async-start | bytes 1179648 | tf_op jit(solution)/shard_map/all_gather | solution.py:45
  152.6 320.0 %reduce-scatter.2.cloned.1.call-start = ((), (), s32[]{:S(2)}) async-start(), calls=%async_computation.4 | async-start | bytes 9175040 | tf_op jit(solution)/shard_map/reduce_scatter | solution.py:53
  320.0 5.9 %copy-start = (f32[2048,512]{0,1:T(8,128)S(1)}, f32[2048,512]{0,1:T(8,128)}, u32[]{:S(2)}) copy-start(f32[2048,512]{0,1:T(8,128)} %all-reduce.4.cloned.1.call-done) | copy-start | bytes 12582916
Sparse Core Ops, SparseCore 0:
  24.1 83.5 all-reduce.3
  117.8 34.7 all-reduce.5
  154.5 23.0 all-gather.1
  344.8 127.7 reduce-scatter.1

commit v3 on v1

--- a/solution.py
+++ b/solution.py
@@ -1,9 +1,75 @@
 import jax
 import jax.numpy as jnp
 from jax import lax
+from jax.experimental import pallas as pl
+from jax.experimental.pallas import tpu as pltpu
 from jax.sharding import PartitionSpec as P
 
 RANK = 512
+BLOCK = 128
+
+
+def _mm(a, b, trans_b=False):
+    dims = (((1,), (1,)), ((), ())) if trans_b else (((1,), (0,)), ((), ()))
+    return lax.dot_general(a, b, dims, precision=lax.Precision.HIGHEST,
+                           preferred_element_type=jnp.float32)
+
+
+def _chol_inv_kernel(g_ref, w_ref, a_ref, d_ref):
+    n = g_ref.shape[0]
+    b = BLOCK
+    a_ref[...] = g_ref[...]
+    rows = lax.broadcasted_iota(jnp.int32, (n, n), 0)
+    cols = lax.broadcasted_iota(jnp.int32, (n, n), 1)
+    w_ref[...] = jnp.where(rows == cols, 1.0, 0.0).astype(jnp.float32)
+    lane = lax.broadcasted_iota(jnp.int32, (1, b), 1)
+    sub = lax.broadcasted_iota(jnp.int32, (b, 1), 0)
+    brow = lax.broadcasted_iota(jnp.int32, (b, b), 0)
+    sub8 = lax.broadcasted_iota(jnp.int32, (8, 1), 0)
+    bcol = lax.broadcasted_iota(jnp.int32, (b, b), 1)
+    for p in range(n // b):
+        lo = p * b
+        d_ref[...] = jnp.where(brow == bcol, 1.0, 0.0).astype(jnp.float32)
+
+        def step(k, carry):
+            base = pl.multiple_of((k // 8) * 8, 8)
+            pick = sub8 == (k - base)
+            slab = a_ref[pl.ds(lo + base, 8), pl.ds(lo, b)]
+            row = jnp.sum(jnp.where(pick, slab, 0.0), axis=0, keepdims=True)
+            diag = jnp.sum(jnp.where(lane == k, row, 0.0), axis=1, keepdims=True)
+            root = jnp.sqrt(diag)
+            lrow = jnp.where(lane >= k, row / root, 0.0)
+            lcol = jnp.transpose(jnp.broadcast_to(lrow, (8, b)))[:, 0:1]
+            blk = a_ref[lo:lo + b, lo:lo + b]
+            a_ref[lo:lo + b, lo:lo + b] = blk - lcol * lrow
+            dslab = d_ref[pl.ds(base, 8), :]
+            wk = jnp.sum(jnp.where(pick, dslab, 0.0), axis=0, keepdims=True) / root
+            strict = jnp.where(sub > k, lcol, 0.0)
+            cur = d_ref[...]
+            d_ref[...] = jnp.where(brow == k, wk, cur - strict * wk)
+            return carry
+
+        lax.fori_loop(0, b, step, 0)
+        winv = d_ref[...]
+        top = w_ref[lo:lo + b, :]
+        newtop = _mm(winv, top)
+        w_ref[lo:lo + b, :] = newtop
+        hi = lo + b
+        if hi < n:
+            panel = _mm(a_ref[hi:, lo:lo + b], winv, trans_b=True)
+            a_ref[hi:, hi:] = a_ref[hi:, hi:] - _mm(panel, panel, trans_b=True)
+            w_ref[hi:, :] = w_ref[hi:, :] - _mm(panel, newtop)
+
+
+def chol_inverse(gram):
+    n = gram.shape[0]
+    return pl.pallas_call(
+        _chol_inv_kernel,
+        out_shape=jax.ShapeDtypeStruct((n, n), jnp.float32),
+        in_specs=[pl.BlockSpec(memory_space=pltpu.VMEM)],
+        out_specs=pl.BlockSpec(memory_space=pltpu.VMEM),
+        scratch_shapes=[pltpu.VMEM((n, n), jnp.float32), pltpu.VMEM((BLOCK, BLOCK), jnp.float32)],
+    )(gram)
 
 
 mix_first = 668265263
@@ -39,10 +105,8 @@
             preferred_element_type=jnp.float32,
         )
         gram = lax.psum(local_gram, "shard")
-        factor = jnp.linalg.cholesky(gram)
-        basis_rows = lax.linalg.triangular_solve(
-            factor, sketch_rows, left_side=False, lower=True, transpose_a=True
-        ).astype(jnp.bfloat16)
+        inverse = chol_inverse(gram)
+        basis_rows = _mm(sketch_rows, inverse, trans_b=True).astype(jnp.bfloat16)
         partial_sum = jnp.dot(basis_rows.T, g, preferred_element_type=jnp.float32)
         outs.append(partial_sum)
     partial_sum = jnp.stack(outs, axis=1)

time: 481 us -> 498 us (1.035); the launches traced: 474 us -> 498 us
  Pallas kernels: 0 us -> 163 us
  other arithmetic: 131 us -> 2.52 us
  local copies, waits for them, and re-layouts: 9.44 us -> 0 us
    pallas_call x0 -> x1, Pallas kernels: none -> 163 us  [chol_inverse(): pl.pallas_call(_chol_inv_kernel, out_shape=jax.ShapeDtypeStruct((n, n), j...]
    another operation x17 -> x0, other arithmetic: 127 us -> none  [the longest x14 87.2 us: body(): factor = jnp.linalg.cholesky(gram)]
    dot_general x0 -> x1, matrix products: none -> 15.2 us  [_mm(): lax.dot_general(a, b, dims, precision=lax.Precision.HIGHEST, preferred_el...]
    another operation x13 -> x0, matrix products: 13.4 us -> none  [the longest x7 11.5 us: body(): lax.linalg.triangular_solve(factor, sketch_rows, left_side=False, lower=T...]
    another operation x17 -> x0, local copies, waits for them, and re-layouts: 7.88 us -> none
where the time goes in v3:
time: 498 us
  waiting for transfers between devices  263 us (53%)
  Pallas kernels  163 us (33%)
  matrix products  55.7 us (11%)
  between operations  13.8 us (3%)
    pallas_call x1, Pallas kernels, chol_inverse(): pl.pallas_call(_chol_inv_kernel, out_shape=jax.ShapeDtypeStruct((n, n), j...  163 us
    reduce_scatter x1, waiting for transfers between devices, body(): lax.psum_scatter(partial_sum, 'shard', scatter_dimension=0, tiled=True)  127 us
    psum x1, waiting for transfers between devices, body(): sketch_rows = lax.psum(partial, 'rep')  83.5 us
    psum x1, waiting for transfers between devices, body(): gram = lax.psum(local_gram, 'shard')  52.1 us
    dot_general x1, matrix products, body(): partial = jnp.dot(g, table, preferred_element_type=jnp.float32)  16.7 us
    dot_general x1, matrix products, _mm(): lax.dot_general(a, b, dims, precision=lax.Precision.HIGHEST, preferred_el...  15.2 us
    dot_general x1, matrix products, body(): partial_sum = jnp.dot(basis_rows.T, g, preferred_element_type=jnp.float32)  13.3 us
    dot_general x1, matrix products, body(): jnp.dot(sketch_rows.T, sketch_rows, precision=lax.Precision.HIGHEST, pref...  10.5 us
  transfers between devices with their start and end apart: 3, of which 3 were waited for; matrix products, arithmetic and copies ran while one was open for 0% of the time, Pallas kernels for 0%

profile of v3, /device:TPU:0, one launch (start us, length us, event | category | flops | bytes accessed | tf_op | source)
XLA Modules:
  0.0 497.8 jit_solution(10330883858400050158)
XLA Ops:
  6.5 0.0 all-reduce.3.cloned.1.call-start
  7.2 16.7 %fusion.24 = f32[2048,512]{0,1:T(8,128)} fusion(bf16[1,2048,3584]{2,1,0:T(8,128)(2,1)} %param.2, s32[]{:T(128)} %bitcast, s32[3584]{0:T(1024)S(1)} %add_multiply_fusion), kind=kOutput, calls=%fused_computation.23 | convolution fusion | flops 7540047872 | bytes 18888708 | tf_op jit(solution)/shard_map/dot_general | solution.py:100
  23.9 0.0 all-reduce.3.cloned.1.call-update
  23.9 0.2 all-reduce.5.cloned.1.call-start
  24.2 83.5 %all-reduce.3.cloned.1.call-done = f32[2048,512]{0,1:T(8,128)} async-done(((f32[2048,512]{0,1:T(8,128)}), f32[2048,512]{0,1:T(8,128)}) %all-reduce.3.cloned.1.call-update) | async-done | bytes 4194320 | tf_op jit(solution)/shard_map/psum | solution.py:101
  107.6 10.5 %fusion.36 = f32[512,512]{1,0:T(8,128)} fusion(f32[2048,512]{0,1:T(8,128)} %all-reduce.3.cloned.1.call-done), kind=kOutput, calls=%fused_computation.33 | convolution fusion | flops 6442450944 | bytes 5242880 | tf_op jit(solution)/shard_map/dot_general | solution.py:102
  118.1 0.0 all-reduce.5.cloned.1.call-update
  118.1 0.0 reduce-scatter.2.cloned.1.call-start
  118.2 52.1 %all-reduce.5.cloned.1.call-done.g_ref = f32[512,512]{1,0:T(8,128)} async-done(((f32[512,512]{1,0:T(8,128)}), f32[512,512]{1,0:T(8,128)}) %all-reduce.5.cloned.1.call-update) | async-done | bytes 1048592 | tf_op jit(solution)/shard_map/psum | solution.py:107
  170.2 162.8 %shard_map.28 = f32[512,512]{1,0:T(8,128)} custom-call(f32[512,512]{1,0:T(8,128)} %all-reduce.5.cloned.1.call-done.g_ref), custom_call_target="tpu_custom_call" | custom-call | tf_op jit(solution)/shard_map/pallas_call | solution.py:66
  333.0 15.2 %convolution_convert_fusion = bf16[2048,512]{1,0:T(8,128)(2,1)S(1)} fusion(f32[2048,512]{0,1:T(8,128)} %all-reduce.3.cloned.1.call-done, f32[512,512]{1,0:T(8,128)} %shard_map.28), kind=kOutput, calls=%fused_computation.24 | convolution fusion | flops 6443499520 | bytes 7340032 | tf_op jit(solution)/shard_map/dot_general | solution.py:14
  348.2 13.3 %fusion.10 = f32[512,1,3584]{2,0,1:T(8,128)} fusion(bf16[2048,512]{1,0:T(8,128)(2,1)S(1)} %convolution_convert_fusion, bf16[1,2048,3584]{2,1,0:T(8,128)(2,1)} %param.2), kind=kOutput, calls=%fused_computation.12 | convolution fusion | flops 7516192768 | bytes 24117248 | tf_op jit(solution)/shard_map/dot_general | solution.py:110
  361.5 0.0 reduce-scatter.2.cloned.1.call-update
  361.6 127.2 %reduce-scatter.2.cloned.1.call-done = f32[128,1,3584]{2,0,1:T(8,128)} async-done(((f32[512,1,3584]{2,0,1:T(8,128)}), f32[128,1,3584]{2,0,1:T(8,128)}) %reduce-scatter.2.cloned.1.call-update) | async-done | bytes 1835024 | tf_op jit(solution)/shard_map/reduce_scatter | solution.py:113
  488.8 2.5 convert_element_type.50
  (1 shorter events, 0.0 us)
Async XLA Ops:
  6.5 101.1 %all-reduce.3.cloned.1.call-start = ((), (), s32[]{:S(2)}) async-start(), calls=%async_computation.1 | async-start | bytes 8388608 | tf_op jit(solution)/shard_map/psum | solution.py:101
  23.9 146.3 %all-reduce.5.cloned.1.call-start = ((), (), s32[]{:S(2)}) async-start(), calls=%async_computation.2 | async-start | bytes 2097152 | tf_op jit(solution)/shard_map/psum | solution.py:107
  118.1 370.7 %reduce-scatter.2.cloned.1.call-start = ((), (), s32[]{:S(2)}) async-start(), calls=%async_computation.3 | async-start | bytes 9175040 | tf_op jit(solution)/shard_map/reduce_scatter | solution.py:113
Sparse Core Ops, SparseCore 0:
  24.1 83.5 all-reduce.2
  118.2 51.9 all-reduce.4
  361.7 127.0 reduce-scatter.1

commit v4 on v1

--- a/solution.py
+++ b/solution.py
@@ -45,9 +45,8 @@
         ).astype(jnp.bfloat16)
         partial_sum = jnp.dot(basis_rows.T, g, preferred_element_type=jnp.float32)
         outs.append(partial_sum)
-    partial_sum = jnp.stack(outs, axis=1)
-    projected = lax.psum_scatter(partial_sum, "shard", scatter_dimension=0, tiled=True)
-    return projected.astype(jnp.bfloat16)
+    partial_sum = jnp.stack(outs, axis=1).astype(jnp.bfloat16)
+    return lax.psum_scatter(partial_sum, "shard", scatter_dimension=0, tiled=True)
 
 
 def solution(mesh):

time: 481 us -> 419 us (0.87)
  waiting for transfers between devices: 263 us -> 203 us
    reduce_scatter x1, waiting for transfers between devices: 127 us -> 68 us  [body(): lax.psum_scatter(partial_sum, 'shard', scatter_dimension=0, tiled=True)]
where the time goes in v4:
time: 419 us; the launch traced here: 411 us
  waiting for transfers between devices  203 us (48%)
  other arithmetic  128 us (31%)
  matrix products  52.9 us (13%)
  between operations  16.9 us (4%)
  local copies, waits for them, and re-layouts  9.44 us (2%)
    another operation x14, other arithmetic, body(): factor = jnp.linalg.cholesky(gram)  87.2 us
    psum x1, waiting for transfers between devices, body(): sketch_rows = lax.psum(partial, 'rep')  83.4 us
    reduce_scatter x1, waiting for transfers between devices, body(): lax.psum_scatter(partial_sum, 'shard', scatter_dimension=0, tiled=True)  68 us
    psum x1, waiting for transfers between devices, body(): gram = lax.psum(local_gram, 'shard')  52 us
    another operation x3, other arithmetic, body(): lax.linalg.triangular_solve(factor, sketch_rows, left_side=False, lower=T...  39.7 us
    dot_general x1, matrix products, body(): partial = jnp.dot(g, table, preferred_element_type=jnp.float32)  16.7 us
    dot_general x1, matrix products, body(): partial_sum = jnp.dot(basis_rows.T, g, preferred_element_type=jnp.float32)  12.6 us
    another operation x7, matrix products, body(): lax.linalg.triangular_solve(factor, sketch_rows, left_side=False, lower=T...  11.5 us
  transfers between devices with their start and end apart: 3, of which 3 were waited for; matrix products, arithmetic and copies ran while one was open for 0% of the time, Pallas kernels for 0%

profile of v4, /device:TPU:0, one launch (start us, length us, event | category | flops | bytes accessed | tf_op | source)
XLA Modules:
  0.0 411.4 jit_solution(13956208684615322948)
XLA Ops:
  7.2 16.7 %fusion.27 = f32[2048,512]{0,1:T(8,128)} fusion(bf16[1,2048,3584]{2,1,0:T(8,128)(2,1)} %param.2, s32[]{:T(128)} %bitcast, s32[3584]{0:T(1024)S(1)} %add_multiply_fusion), kind=kOutput, calls=%fused_computation.26 | convolution fusion | flops 7540047872 | bytes 18888708 | tf_op jit(solution)/shard_map/dot_general | solution.py:34
  23.9 0.3 all-reduce.6.cloned.1.call-start
  24.3 83.4 %all-reduce.4.cloned.1.call-done = f32[2048,512]{0,1:T(8,128)} async-done(((f32[2048,512]{0,1:T(8,128)}), f32[2048,512]{0,1:T(8,128)}) %all-reduce.4.cloned.1.call-update) | async-done | bytes 4194320 | tf_op jit(solution)/shard_map/psum | solution.py:35
  107.6 10.2 %fusion.84 = f32[512,512]{0,1:T(8,128)} fusion(f32[2048,512]{0,1:T(8,128)} %all-reduce.4.cloned.1.call-done), kind=kOutput, calls=%fused_computation.111 | convolution fusion | flops 6442450944 | bytes 5242880 | tf_op jit(solution)/shard_map/dot_general | solution.py:36
  118.0 52.0 %all-reduce.6.cloned.1.call-done = f32[512,512]{0,1:T(8,128)} async-done(((f32[512,512]{0,1:T(8,128)}), f32[512,512]{0,1:T(8,128)}) %all-reduce.6.cloned.1.call-update) | async-done | bytes 1048592 | tf_op jit(solution)/shard_map/psum | solution.py:41
  170.0 1.6 copy.6
  171.6 1.4 fusion.53
  173.0 11.7 %cholesky.104 = f32[128,128]{1,0:T(8,128)S(1)} custom-call(f32[128,128]{1,0:T(8,128)S(1)} %cholesky.266), custom_call_target="Cholesky" | custom-call | tf_op jit(solution)/shard_map/jit(cholesky)/cholesky | solution.py:42
  184.8 9.8 %custom-call.30 = f32[1,128,128]{1,2,0:T(8,128)S(1)} custom-call(f32[1,128,128]{2,1,0:T(8,128)S(1)} %get-tuple-element.32), custom_call_target="InvertDiagBlocksLowerTriangular" | custom-call | tf_op jit(solution)/shard_map/jit(cholesky)/cholesky | solution.py:42
  194.6 0.1 cholesky.224
  194.7 0.3 constant_dynamic-update-slice_fusion.3
  195.1 0.3 convolution_subtract_fusion.2
  195.4 11.7 %cholesky.217 = f32[128,128]{1,0:T(8,128)S(1)} custom-call(f32[128,128]{1,0:T(8,128)S(1)} %cholesky.270), custom_call_target="Cholesky" | custom-call | tf_op jit(solution)/shard_map/jit(cholesky)/cholesky | solution.py:42
  207.2 18.5 %custom-call.31 = f32[1,128,128]{1,2,0:T(8,128)S(1)} custom-call(f32[1,128,128]{2,1,0:T(8,128)S(1)} %get-tuple-element.29), custom_call_target="InvertDiagBlocksLowerTriangular" | custom-call | tf_op jit(solution)/shard_map/jit(cholesky)/cholesky | solution.py:42
  225.7 0.3 convolution_dynamic-update-slice_fusion
  225.9 0.4 convolution_subtract_fusion.3
  226.3 11.7 %cholesky.238 = f32[128,128]{1,0:T(8,128)S(1)} custom-call(f32[128,128]{1,0:T(8,128)S(1)} %cholesky.275), custom_call_target="Cholesky" | custom-call | tf_op jit(solution)/shard_map/jit(cholesky)/cholesky | solution.py:42
  238.1 0.7 compare_reduce_fusion.1
  238.7 9.8 %custom-call.32 = f32[1,128,128]{1,2,0:T(8,128)S(1)} custom-call(f32[1,128,128]{2,1,0:T(8,128)S(1)} %get-tuple-element.26), custom_call_target="InvertDiagBlocksLowerTriangular" | custom-call | tf_op jit(solution)/shard_map/jit(cholesky)/cholesky | solution.py:42
  248.6 0.2 convolution_dynamic-update-slice_fusion.1
  248.8 0.4 convolution_subtract_fusion.4
  249.2 11.7 %cholesky.255 = f32[128,128]{1,0:T(8,128)S(1)} custom-call(f32[128,128]{1,0:T(8,128)S(1)} %convolution_subtract_fusion.4), custom_call_target="Cholesky" | custom-call | tf_op jit(solution)/shard_map/jit(cholesky)/cholesky | solution.py:42
  260.9 0.7 compare_reduce_fusion
  261.6 0.7 compare_reduce_fusion.2
  264.8 0.3 select_select_fusion
  265.1 7.8 %while.1 = (s32[]{:T(128)}, f32[512,512]{1,0:T(8,128)S(1)}, s32[4,2]{0,1:T(2,128)S(1)}, f32[4,128,128]{2,1,0:T(8,128)S(1)}, s32[]{:T(128)}) while((s32[]{:T(128)}, f32[512,512]{1,0:T(8,128)S(1)}, s32[4,2]{0,1:T(2,128)S(1)}, f32[4,128,128]{2,1,0:T(8,128)S(1)}, s32[]{:T(128)}) %tuple.30), condition=%wide.while_cond, body=%wide.while_body.sunk | while | flops 2 | bytes 131189 | solution.py:43
  265.2 0.1 constant_dynamic-slice_fusion.2
  265.2 0.5 fusion.93
  265.8 1.3 bitcast_dynamic-update-slice_fusion.2
  267.1 0.1 constant_dynamic-slice_fusion.2
  267.2 0.5 fusion.93
  267.7 1.3 bitcast_dynamic-update-slice_fusion.2
  269.1 0.1 constant_dynamic-slice_fusion.2
  269.1 0.5 fusion.93
  269.7 1.3 bitcast_dynamic-update-slice_fusion.2
  271.0 0.1 constant_dynamic-slice_fusion.2
  271.1 0.5 fusion.93
  271.6 1.3 bitcast_dynamic-update-slice_fusion.2
  273.0 39.3 %custom-call.33 = f32[4,128,128]{1,2,0:T(8,128)S(1)} custom-call(f32[4,128,128]{2,1,0:T(8,128)S(1)} %get-tuple-element.12), custom_call_target="InvertDiagBlocksLowerTriangular" | custom-call | tf_op jit(solution)/shard_map/triangular_solve | solution.py:43
  312.3 2.5 fusion.83
  314.8 2.3 convolution_subtract_fusion.1
  317.1 1.1 fusion.82
  318.2 1.3 convolution_subtract_fusion
  319.5 1.1 fusion.81
  320.6 2.2 fusion.38
  322.8 1.1 convolution_convert_fusion
  323.9 12.6 %fusion.13 = bf16[512,1,3584]{2,0,1:T(8,128)(2,1)} fusion(bf16[1,2048,3584]{2,1,0:T(8,128)(2,1)} %param.2, bf16[2048,128]{0,1:T(8,128)(2,1)S(1)} %convolution_convert_fusion, bf16[2048,128]{0,1:T(8,128)(2,1)S(1)} %get-tuple-element.35, bf16[2048,128]{0,1:T(8,128)(2,1)S(1)} %get-tuple-element.37, bf16[2048,128]{0,1:T(8,128)(2,1)S(1)} %get-tuple-element.39), kind=kOutput, calls=%fused_computation.15 | convolution fusion | flops 7526416384 | bytes 20447232 | tf_op jit(solution)/shard_map/dot_general | solution.py:46
  336.5 68.0 %reduce-scatter.2.cloned.1.call-done = bf16[128,1,3584]{2,0,1:T(8,128)(2,1)} async-done(((bf16[512,1,3584]{2,0,1:T(8,128)(2,1)}), bf16[128,1,3584]{2,0,1:T(8,128)(2,1)}) %reduce-scatter.2.cloned.1.call-update) | async-done | bytes 917520 | tf_op jit(solution)/shard_map/reduce_scatter | solution.py:49
  (18 shorter events, 0.3 us)
Async XLA Ops:
  6.5 101.1 %all-reduce.4.cloned.1.call-start = ((), (), s32[]{:S(2)}) async-start(), calls=%async_computation.1 | async-start | bytes 8388608 | tf_op jit(solution)/shard_map/psum | solution.py:35
  23.9 146.1 %all-reduce.6.cloned.1.call-start = ((), (), s32[]{:S(2)}) async-start(), calls=%async_computation.2 | async-start | bytes 2097152 | tf_op jit(solution)/shard_map/psum | solution.py:41
  117.9 286.6 %reduce-scatter.2.cloned.1.call-start = ((), (), s32[]{:S(2)}) async-start(), calls=%async_computation.3 | async-start | bytes 4587520 | tf_op jit(solution)/shard_map/reduce_scatter | solution.py:49
  312.3 5.9 %copy-start = (f32[2048,512]{0,1:T(8,128)S(1)}, f32[2048,512]{0,1:T(8,128)}, u32[]{:S(2)}) copy-start(f32[2048,512]{0,1:T(8,128)} %all-reduce.4.cloned.1.call-done) | copy-start | bytes 12582916
Sparse Core Ops, SparseCore 0:
  24.1 83.5 all-reduce.3
  118.0 51.9 all-reduce.5
  336.6 67.8 reduce-scatter.1

commit v5 on v3

--- a/solution.py
+++ b/solution.py
@@ -15,42 +15,36 @@
                            preferred_element_type=jnp.float32)
 
 
-def _chol_inv_kernel(g_ref, w_ref, a_ref, d_ref):
+def _chol_inv_kernel(g_ref, w_ref, a_ref):
     n = g_ref.shape[0]
     b = BLOCK
     a_ref[...] = g_ref[...]
     rows = lax.broadcasted_iota(jnp.int32, (n, n), 0)
     cols = lax.broadcasted_iota(jnp.int32, (n, n), 1)
     w_ref[...] = jnp.where(rows == cols, 1.0, 0.0).astype(jnp.float32)
-    lane = lax.broadcasted_iota(jnp.int32, (1, b), 1)
+    arow = lax.broadcasted_iota(jnp.int32, (b, 2 * b), 0)
+    acol = lax.broadcasted_iota(jnp.int32, (b, 2 * b), 1)
+    bcol = lax.broadcasted_iota(jnp.int32, (b, b), 1)
     sub = lax.broadcasted_iota(jnp.int32, (b, 1), 0)
-    brow = lax.broadcasted_iota(jnp.int32, (b, b), 0)
-    sub8 = lax.broadcasted_iota(jnp.int32, (8, 1), 0)
-    bcol = lax.broadcasted_iota(jnp.int32, (b, b), 1)
+    eye = jnp.where(arow + b == acol, 1.0, 0.0).astype(jnp.float32)
     for p in range(n // b):
         lo = p * b
-        d_ref[...] = jnp.where(brow == bcol, 1.0, 0.0).astype(jnp.float32)
+        blk = a_ref[lo:lo + b, lo:lo + b]
+        aug = jnp.where(acol < b, jnp.concatenate([blk, blk], axis=1), eye)
 
-        def step(k, carry):
-            base = pl.multiple_of((k // 8) * 8, 8)
-            pick = sub8 == (k - base)
-            slab = a_ref[pl.ds(lo + base, 8), pl.ds(lo, b)]
-            row = jnp.sum(jnp.where(pick, slab, 0.0), axis=0, keepdims=True)
-            diag = jnp.sum(jnp.where(lane == k, row, 0.0), axis=1, keepdims=True)
-            root = jnp.sqrt(diag)
-            lrow = jnp.where(lane >= k, row / root, 0.0)
-            lcol = jnp.transpose(jnp.broadcast_to(lrow, (8, b)))[:, 0:1]
-            blk = a_ref[lo:lo + b, lo:lo + b]
-            a_ref[lo:lo + b, lo:lo + b] = blk - lcol * lrow
-            dslab = d_ref[pl.ds(base, 8), :]
-            wk = jnp.sum(jnp.where(pick, dslab, 0.0), axis=0, keepdims=True) / root
-            strict = jnp.where(sub > k, lcol, 0.0)
-            cur = d_ref[...]
-            d_ref[...] = jnp.where(brow == k, wk, cur - strict * wk)
-            return carry
+        def step(k, aug):
+            row = jnp.sum(jnp.where(arow == k, aug, 0.0), axis=0, keepdims=True)
+            left = aug[:, :b]
+            col = jnp.sum(jnp.where(bcol == k, left, 0.0), axis=1, keepdims=True)
+            diag = jnp.sum(jnp.where(sub == k, col, 0.0), axis=0, keepdims=True)
+            inv = 1.0 / jnp.sqrt(diag)
+            lrow = row * inv
+            strict = jnp.where(sub > k, col * inv, 0.0)
+            upd = aug - strict * lrow
+            return jnp.where((arow == k) & (acol >= b), lrow, upd)
 
-        lax.fori_loop(0, b, step, 0)
-        winv = d_ref[...]
+        aug = lax.fori_loop(0, b, step, aug, unroll=4)
+        winv = aug[:, b:]
         top = w_ref[lo:lo + b, :]
         newtop = _mm(winv, top)
         w_ref[lo:lo + b, :] = newtop
@@ -68,7 +62,7 @@
         out_shape=jax.ShapeDtypeStruct((n, n), jnp.float32),
         in_specs=[pl.BlockSpec(memory_space=pltpu.VMEM)],
         out_specs=pl.BlockSpec(memory_space=pltpu.VMEM),
-        scratch_shapes=[pltpu.VMEM((n, n), jnp.float32), pltpu.VMEM((BLOCK, BLOCK), jnp.float32)],
+        scratch_shapes=[pltpu.VMEM((n, n), jnp.float32)],
     )(gram)
 
 
@@ -105,13 +99,12 @@
             preferred_element_type=jnp.float32,
         )
         gram = lax.psum(local_gram, "shard")
-        inverse = chol_inverse(gram)
+        inverse = chol_inverse(0.5 * (gram + gram.T))
         basis_rows = _mm(sketch_rows, inverse, trans_b=True).astype(jnp.bfloat16)
         partial_sum = jnp.dot(basis_rows.T, g, preferred_element_type=jnp.float32)
         outs.append(partial_sum)
-    partial_sum = jnp.stack(outs, axis=1)
-    projected = lax.psum_scatter(partial_sum, "shard", scatter_dimension=0, tiled=True)
-    return projected.astype(jnp.bfloat16)
+    partial_sum = jnp.stack(outs, axis=1).astype(jnp.bfloat16)
+    return lax.psum_scatter(partial_sum, "shard", scatter_dimension=0, tiled=True)
 
 
 def solution(mesh):

time: 498 us -> 347 us (0.70)
  Pallas kernels: 163 us -> 70.5 us
  waiting for transfers between devices: 263 us -> 204 us
    pallas_call x1, Pallas kernels: 163 us -> 70.5 us  [chol_inverse(): pl.pallas_call(_chol_inv_kernel, out_shape=jax.ShapeDtypeStruct((n, n), j...]
    reduce_scatter x1, waiting for transfers between devices: 127 us -> 68 us  [body(): lax.psum_scatter(partial_sum, 'shard', scatter_dimension=0, tiled=True)]
where the time goes in v5:
time: 347 us
  waiting for transfers between devices  204 us (59%)
  Pallas kernels  70.5 us (20%)
  matrix products  55.1 us (16%)
  between operations  13.8 us (4%)
    psum x1, waiting for transfers between devices, body(): sketch_rows = lax.psum(partial, 'rep')  83.5 us
    pallas_call x1, Pallas kernels, chol_inverse(): pl.pallas_call(_chol_inv_kernel, out_shape=jax.ShapeDtypeStruct((n, n), j...  70.5 us
    reduce_scatter x1, waiting for transfers between devices, body(): lax.psum_scatter(partial_sum, 'shard', scatter_dimension=0, tiled=True)  68 us
    psum x1, waiting for transfers between devices, body(): gram = lax.psum(local_gram, 'shard')  52.1 us
    dot_general x1, matrix products, body(): partial = jnp.dot(g, table, preferred_element_type=jnp.float32)  16.7 us
    dot_general x1, matrix products, _mm(): lax.dot_general(a, b, dims, precision=lax.Precision.HIGHEST, preferred_el...  15.2 us
    dot_general x1, matrix products, body(): partial_sum = jnp.dot(basis_rows.T, g, preferred_element_type=jnp.float32)  12.8 us
    dot_general x1, matrix products, body(): jnp.dot(sketch_rows.T, sketch_rows, precision=lax.Precision.HIGHEST, pref...  10.4 us
  transfers between devices with their start and end apart: 3, of which 3 were waited for; matrix products, arithmetic and copies ran while one was open for 0% of the time, Pallas kernels for 0%

profile of v5, /device:TPU:0, one launch (start us, length us, event | category | flops | bytes accessed | tf_op | source)
XLA Modules:
  0.0 347.2 jit_solution(735273621560186914)
XLA Ops:
  6.5 0.0 all-reduce.3.cloned.1.call-start
  7.2 16.7 %fusion.27 = f32[2048,512]{0,1:T(8,128)} fusion(bf16[1,2048,3584]{2,1,0:T(8,128)(2,1)} %param.2, s32[]{:T(128)} %bitcast, s32[3584]{0:T(1024)S(1)} %add_multiply_fusion), kind=kOutput, calls=%fused_computation.24 | convolution fusion | flops 7540047872 | bytes 18888708 | tf_op jit(solution)/shard_map/dot_general | solution.py:94
  23.9 0.0 all-reduce.3.cloned.1.call-update
  23.9 0.2 all-reduce.5.cloned.1.call-start
  24.2 83.5 %all-reduce.3.cloned.1.call-done = f32[2048,512]{0,1:T(8,128)} async-done(((f32[2048,512]{0,1:T(8,128)}), f32[2048,512]{0,1:T(8,128)}) %all-reduce.3.cloned.1.call-update) | async-done | bytes 4194320 | tf_op jit(solution)/shard_map/psum | solution.py:95
  107.6 10.4 %fusion.40 = f32[512,512]{0,1:T(8,128)} fusion(f32[2048,512]{0,1:T(8,128)} %all-reduce.3.cloned.1.call-done), kind=kOutput, calls=%fused_computation.36 | convolution fusion | flops 6442450944 | bytes 5242880 | tf_op jit(solution)/shard_map/dot_general | solution.py:96
  118.0 0.0 all-reduce.5.cloned.1.call-update
  118.0 0.0 reduce-scatter.2.cloned.1.call-start
  118.1 52.1 %all-reduce.5.cloned.1.call-done = f32[512,512]{0,1:T(8,128)} async-done(((f32[512,512]{0,1:T(8,128)}), f32[512,512]{0,1:T(8,128)}) %all-reduce.5.cloned.1.call-update) | async-done | bytes 1048592 | tf_op jit(solution)/shard_map/psum | solution.py:101
  170.2 1.6 copy.6
  171.7 2.5 fusion.32.g_ref
  174.2 70.5 %shard_map.28 = f32[512,512]{1,0:T(8,128)} custom-call(f32[512,512]{1,0:T(8,128)} %fusion.32.g_ref), custom_call_target="tpu_custom_call" | custom-call | tf_op jit(solution)/shard_map/pallas_call | solution.py:60
  244.7 15.2 %convolution_convert_fusion = bf16[2048,512]{1,0:T(8,128)(2,1)S(1)} fusion(f32[2048,512]{0,1:T(8,128)} %all-reduce.3.cloned.1.call-done, f32[512,512]{1,0:T(8,128)} %shard_map.28), kind=kOutput, calls=%fused_computation.25 | convolution fusion | flops 6443499520 | bytes 7340032 | tf_op jit(solution)/shard_map/dot_general | solution.py:14
  259.9 12.8 %fusion.13 = bf16[512,1,3584]{2,0,1:T(8,128)(2,1)} fusion(bf16[2048,512]{1,0:T(8,128)(2,1)S(1)} %convolution_convert_fusion, bf16[1,2048,3584]{2,1,0:T(8,128)(2,1)} %param.2), kind=kOutput, calls=%fused_computation.13 | convolution fusion | flops 7518027776 | bytes 20447232 | tf_op jit(solution)/shard_map/dot_general | solution.py:104
  272.7 0.0 reduce-scatter.2.cloned.1.call-update
  272.7 68.0 %reduce-scatter.2.cloned.1.call-done = bf16[128,1,3584]{2,0,1:T(8,128)(2,1)} async-done(((bf16[512,1,3584]{2,0,1:T(8,128)(2,1)}), bf16[128,1,3584]{2,0,1:T(8,128)(2,1)}) %reduce-scatter.2.cloned.1.call-update) | async-done | bytes 917520 | tf_op jit(solution)/shard_map/reduce_scatter | solution.py:107
  (1 shorter events, 0.0 us)
Async XLA Ops:
  6.5 101.1 %all-reduce.3.cloned.1.call-start = ((), (), s32[]{:S(2)}) async-start(), calls=%async_computation.1 | async-start | bytes 8388608 | tf_op jit(solution)/shard_map/psum | solution.py:95
  23.9 146.2 %all-reduce.5.cloned.1.call-start = ((), (), s32[]{:S(2)}) async-start(), calls=%async_computation.2 | async-start | bytes 2097152 | tf_op jit(solution)/shard_map/psum | solution.py:101
  118.0 222.6 %reduce-scatter.2.cloned.1.call-start = ((), (), s32[]{:S(2)}) async-start(), calls=%async_computation.3 | async-start | bytes 4587520 | tf_op jit(solution)/shard_map/reduce_scatter | solution.py:107
Sparse Core Ops, SparseCore 0:
  24.1 83.5 all-reduce.2
  118.2 51.9 all-reduce.4
  272.8 67.8 reduce-scatter.1

commit v6 on v5

--- a/solution.py
+++ b/solution.py
@@ -9,9 +9,9 @@
 BLOCK = 128
 
 
-def _mm(a, b, trans_b=False):
+def _mm(a, b, trans_b=False, precision=lax.Precision.HIGHEST):
     dims = (((1,), (1,)), ((), ())) if trans_b else (((1,), (0,)), ((), ()))
-    return lax.dot_general(a, b, dims, precision=lax.Precision.HIGHEST,
+    return lax.dot_general(a, b, dims, precision=precision,
                            preferred_element_type=jnp.float32)
 
 
@@ -84,6 +84,27 @@
     return (2.0 * unit - 1.0).astype(jnp.bfloat16)
 
 
+def symmetric_psum(local, axis):
+    b = BLOCK
+    nb = local.shape[0] // b
+    pairs = [(i, j) for i in range(nb) for j in range(i + 1)]
+    packed = jnp.stack([local[i * b:(i + 1) * b, j * b:(j + 1) * b] for i, j in pairs])
+    packed = lax.psum(packed, axis)
+    blocks = {pair: packed[t] for t, pair in enumerate(pairs)}
+    grid = []
+    for i in range(nb):
+        line = []
+        for j in range(nb):
+            if i == j:
+                line.append(0.5 * (blocks[(i, i)] + blocks[(i, i)].T))
+            elif i > j:
+                line.append(blocks[(i, j)])
+            else:
+                line.append(blocks[(j, i)].T)
+        grid.append(line)
+    return jnp.block(grid)
+
+
 def body(grads, seeds):
     mats, depth, width = grads.shape
     col0 = lax.axis_index("rep") * width
@@ -98,9 +119,11 @@
             precision=lax.Precision.HIGHEST,
             preferred_element_type=jnp.float32,
         )
-        gram = lax.psum(local_gram, "shard")
-        inverse = chol_inverse(0.5 * (gram + gram.T))
-        basis_rows = _mm(sketch_rows, inverse, trans_b=True).astype(jnp.bfloat16)
+        gram = symmetric_psum(local_gram, "shard")
+        inverse = chol_inverse(gram)
+        basis_rows = _mm(
+            sketch_rows, inverse, trans_b=True, precision=lax.Precision.HIGH
+        ).astype(jnp.bfloat16)
         partial_sum = jnp.dot(basis_rows.T, g, preferred_element_type=jnp.float32)
         outs.append(partial_sum)
     partial_sum = jnp.stack(outs, axis=1).astype(jnp.bfloat16)

time: 347 us -> 332 us (0.957)
  waiting for transfers between devices: 204 us -> 192 us
  matrix products: 55.1 us -> 48 us
    psum x1, waiting for transfers between devices: 52.1 us -> 40.5 us  [symmetric_psum(): packed = lax.psum(packed, axis)]
    dot_general x1, matrix products: 15.2 us -> 9.17 us  [_mm(): lax.dot_general(a, b, dims, precision=precision, preferred_element_type=j...]
where the time goes in v6:
time: 332 us; the launch traced here: 331 us
  waiting for transfers between devices  192 us (58%)
  Pallas kernels  70.5 us (21%)
  matrix products  48 us (14%)
  between operations  14 us (4%)
  local copies, waits for them, and re-layouts  3.37 us (1%)
    psum x1, waiting for transfers between devices, body(): sketch_rows = lax.psum(partial, 'rep')  83.5 us
    pallas_call x1, Pallas kernels, chol_inverse(): pl.pallas_call(_chol_inv_kernel, out_shape=jax.ShapeDtypeStruct((n, n), j...  70.5 us
    reduce_scatter x1, waiting for transfers between devices, body(): lax.psum_scatter(partial_sum, 'shard', scatter_dimension=0, tiled=True)  68.2 us
    psum x1, waiting for transfers between devices, symmetric_psum(): packed = lax.psum(packed, axis)  40.5 us
    dot_general x1, matrix products, body(): partial = jnp.dot(g, table, preferred_element_type=jnp.float32)  16.7 us
    dot_general x1, matrix products, body(): partial_sum = jnp.dot(basis_rows.T, g, preferred_element_type=jnp.float32)  12.7 us
    dot_general x1, matrix products, body(): jnp.dot(sketch_rows.T, sketch_rows, precision=lax.Precision.HIGHEST, pref...  9.42 us
    dot_general x1, matrix products, _mm(): lax.dot_general(a, b, dims, precision=precision, preferred_element_type=j...  9.17 us
  transfers between devices with their start and end apart: 3, of which 3 were waited for; matrix products, arithmetic and copies ran while one was open for 0% of the time, Pallas kernels for 0%

profile of v6, /device:TPU:0, one launch (start us, length us, event | category | flops | bytes accessed | tf_op | source)
XLA Modules:
  0.0 331.4 jit_solution(3080295610358671804)
XLA Ops:
  6.5 0.0 all-reduce.3.cloned.1.call-start
  7.2 16.7 %fusion.27 = f32[2048,512]{0,1:T(8,128)} fusion(bf16[1,2048,3584]{2,1,0:T(8,128)(2,1)} %param.2, s32[]{:T(128)} %bitcast, s32[3584]{0:T(1024)S(1)} %add_multiply_fusion), kind=kOutput, calls=%fused_computation.24 | convolution fusion | flops 7540047872 | bytes 18888708 | tf_op jit(solution)/shard_map/dot_general | solution.py:115
  23.9 0.0 all-reduce.3.cloned.1.call-update
  23.9 0.2 all-reduce.5.cloned.1.call-start
  24.2 83.5 %all-reduce.3.cloned.1.call-done = f32[2048,512]{0,1:T(8,128)} async-done(((f32[2048,512]{0,1:T(8,128)}), f32[2048,512]{0,1:T(8,128)}) %all-reduce.3.cloned.1.call-update) | async-done | bytes 4194320 | tf_op jit(solution)/shard_map/psum | solution.py:116
  107.6 9.4 %fusion.52 = f32[512,512]{0,1:T(8,128)S(1)} fusion(f32[2048,512]{0,1:T(8,128)} %all-reduce.3.cloned.1.call-done), kind=kOutput, calls=%fused_computation.74 | convolution fusion | flops 6442450944 | bytes 5242880 | tf_op jit(solution)/shard_map/dot_general | solution.py:117
  117.2 0.0 copy-start
  117.3 0.8 copy-done
  118.1 0.0 all-reduce.5.cloned.1.call-update
  118.1 0.0 reduce-scatter.2.cloned.1.call-start
  118.2 40.5 %all-reduce.5.cloned.1.call-done = f32[10,128,128]{1,2,0:T(8,128)} async-done(((f32[10,128,128]{1,2,0:T(8,128)}), f32[10,128,128]{1,2,0:T(8,128)}) %all-reduce.5.cloned.1.call-update) | async-done | bytes 655376 | tf_op jit(solution)/shard_map/psum | solution.py:92
  158.7 1.2 fusion.51
  159.9 0.1 copy.54
  160.0 0.1 copy.56
  160.1 0.1 copy.55
  160.2 0.1 copy.57
  160.3 0.1 copy.50
  160.4 0.1 copy.47
  160.5 0.1 copy.44
  160.6 0.1 copy.45
  160.7 0.1 copy.51
  160.8 0.1 copy.48
  160.9 0.9 fusion.42
  161.8 0.1 copy.49
  161.9 0.1 copy.46
  162.1 0.1 copy.52
  162.2 0.9 fusion.43
  163.1 1.1 maximum_maximum_fusion.g_ref
  164.2 70.5 %shard_map.28 = f32[512,512]{1,0:T(8,128)} custom-call(f32[512,512]{1,0:T(8,128)} %maximum_maximum_fusion.g_ref), custom_call_target="tpu_custom_call" | custom-call | tf_op jit(solution)/shard_map/pallas_call | solution.py:60
  234.7 9.2 %convolution_convert_fusion = bf16[2048,512]{1,0:T(8,128)(2,1)S(1)} fusion(f32[2048,512]{0,1:T(8,128)} %all-reduce.3.cloned.1.call-done, f32[512,512]{1,0:T(8,128)} %shard_map.28), kind=kOutput, calls=%fused_computation.25 | convolution fusion | flops 3222274048 | bytes 7340032 | tf_op jit(solution)/shard_map/dot_general | solution.py:14
  243.8 12.7 %fusion.13 = bf16[512,1,3584]{2,0,1:T(8,128)(2,1)} fusion(bf16[2048,512]{1,0:T(8,128)(2,1)S(1)} %convolution_convert_fusion, bf16[1,2048,3584]{2,1,0:T(8,128)(2,1)} %param.2), kind=kOutput, calls=%fused_computation.13 | convolution fusion | flops 7518027776 | bytes 20447232 | tf_op jit(solution)/shard_map/dot_general | solution.py:127
  256.6 0.0 reduce-scatter.2.cloned.1.call-update
  256.6 68.2 %reduce-scatter.2.cloned.1.call-done = bf16[128,1,3584]{2,0,1:T(8,128)(2,1)} async-done(((bf16[512,1,3584]{2,0,1:T(8,128)(2,1)}), bf16[128,1,3584]{2,0,1:T(8,128)(2,1)}) %reduce-scatter.2.cloned.1.call-update) | async-done | bytes 917520 | tf_op jit(solution)/shard_map/reduce_scatter | solution.py:130
  (13 shorter events, 0.1 us)
Async XLA Ops:
  6.5 101.1 %all-reduce.3.cloned.1.call-start = ((), (), s32[]{:S(2)}) async-start(), calls=%async_computation.1 | async-start | bytes 8388608 | tf_op jit(solution)/shard_map/psum | solution.py:116
  23.9 134.7 %all-reduce.5.cloned.1.call-start = ((), (), s32[]{:S(2)}) async-start(), calls=%async_computation.2 | async-start | bytes 1310720 | tf_op jit(solution)/shard_map/psum | solution.py:92
  117.2 0.8 copy-start
  118.1 206.7 %reduce-scatter.2.cloned.1.call-start = ((), (), s32[]{:S(2)}) async-start(), calls=%async_computation.3 | async-start | bytes 4587520 | tf_op jit(solution)/shard_map/reduce_scatter | solution.py:130
Sparse Core Ops, SparseCore 0:
  24.1 83.5 all-reduce.2
  118.2 40.4 all-reduce.4
  256.7 68.0 reduce-scatter.1

commit v7 on v5

--- a/solution.py
+++ b/solution.py
@@ -9,16 +9,24 @@
 BLOCK = 128
 
 
-def _mm(a, b, trans_b=False):
+def _mm(a, b, trans_b=False, precision=lax.Precision.HIGHEST):
     dims = (((1,), (1,)), ((), ())) if trans_b else (((1,), (0,)), ((), ()))
-    return lax.dot_general(a, b, dims, precision=lax.Precision.HIGHEST,
+    return lax.dot_general(a, b, dims, precision=precision,
                            preferred_element_type=jnp.float32)
 
 
+def _tri(i, j):
+    return i * (i + 1) // 2 + j
+
+
 def _chol_inv_kernel(g_ref, w_ref, a_ref):
-    n = g_ref.shape[0]
     b = BLOCK
+    n = w_ref.shape[0]
+    nb = n // b
     a_ref[...] = g_ref[...]
+    for i in range(nb):
+        d = g_ref[_tri(i, i)]
+        a_ref[_tri(i, i)] = 0.5 * (d + d.T)
     rows = lax.broadcasted_iota(jnp.int32, (n, n), 0)
     cols = lax.broadcasted_iota(jnp.int32, (n, n), 1)
     w_ref[...] = jnp.where(rows == cols, 1.0, 0.0).astype(jnp.float32)
@@ -27,9 +35,9 @@
     bcol = lax.broadcasted_iota(jnp.int32, (b, b), 1)
     sub = lax.broadcasted_iota(jnp.int32, (b, 1), 0)
     eye = jnp.where(arow + b == acol, 1.0, 0.0).astype(jnp.float32)
-    for p in range(n // b):
+    for p in range(nb):
         lo = p * b
-        blk = a_ref[lo:lo + b, lo:lo + b]
+        blk = a_ref[_tri(p, p)]
         aug = jnp.where(acol < b, jnp.concatenate([blk, blk], axis=1), eye)
 
         def step(k, aug):
@@ -45,25 +53,28 @@
 
         aug = lax.fori_loop(0, b, step, aug, unroll=4)
         winv = aug[:, b:]
-        top = w_ref[lo:lo + b, :]
-        newtop = _mm(winv, top)
+        newtop = _mm(winv, w_ref[lo:lo + b, :])
         w_ref[lo:lo + b, :] = newtop
-        hi = lo + b
-        if hi < n:
-            panel = _mm(a_ref[hi:, lo:lo + b], winv, trans_b=True)
-            a_ref[hi:, hi:] = a_ref[hi:, hi:] - _mm(panel, panel, trans_b=True)
-            w_ref[hi:, :] = w_ref[hi:, :] - _mm(panel, newtop)
+        panels = {i: _mm(a_ref[_tri(i, p)], winv, trans_b=True) for i in range(p + 1, nb)}
+        for i in range(p + 1, nb):
+            for j in range(p + 1, i + 1):
+                a_ref[_tri(i, j)] = a_ref[_tri(i, j)] - _mm(panels[i], panels[j], trans_b=True)
+            w_ref[i * b:(i + 1) * b, :] = w_ref[i * b:(i + 1) * b, :] - _mm(panels[i], newtop)
 
 
-def chol_inverse(gram):
-    n = gram.shape[0]
+def chol_inverse(packed):
+    t = packed.shape[0]
+    nb = 1
+    while nb * (nb + 1) // 2 < t:
+        nb += 1
+    n = nb * BLOCK
     return pl.pallas_call(
         _chol_inv_kernel,
         out_shape=jax.ShapeDtypeStruct((n, n), jnp.float32),
         in_specs=[pl.BlockSpec(memory_space=pltpu.VMEM)],
         out_specs=pl.BlockSpec(memory_space=pltpu.VMEM),
-        scratch_shapes=[pltpu.VMEM((n, n), jnp.float32)],
-    )(gram)
+        scratch_shapes=[pltpu.VMEM(packed.shape, jnp.float32)],
+    )(packed)
 
 
 mix_first = 668265263
@@ -84,6 +95,14 @@
     return (2.0 * unit - 1.0).astype(jnp.bfloat16)
 
 
+def lower_blocks_psum(local, axis):
+    b = BLOCK
+    nb = local.shape[0] // b
+    pairs = [(i, j) for i in range(nb) for j in range(i + 1)]
+    packed = jnp.stack([local[i * b:(i + 1) * b, j * b:(j + 1) * b] for i, j in pairs])
+    return lax.psum(packed, axis)
+
+
 def body(grads, seeds):
     mats, depth, width = grads.shape
     col0 = lax.axis_index("rep") * width
@@ -95,12 +114,14 @@
         sketch_rows = lax.psum(partial, "rep")
         local_gram = jnp.dot(
             sketch_rows.T, sketch_rows,
-            precision=lax.Precision.HIGHEST,
+            precision=lax.Precision.HIGH,
             preferred_element_type=jnp.float32,
         )
-        gram = lax.psum(local_gram, "shard")
-        inverse = chol_inverse(0.5 * (gram + gram.T))
-        basis_rows = _mm(sketch_rows, inverse, trans_b=True).astype(jnp.bfloat16)
+        gram = lower_blocks_psum(local_gram, "shard")
+        inverse = chol_inverse(gram)
+        basis_rows = _mm(
+            sketch_rows, inverse, trans_b=True, precision=lax.Precision.HIGH
+        ).astype(jnp.bfloat16)
         partial_sum = jnp.dot(basis_rows.T, g, preferred_element_type=jnp.float32)
         outs.append(partial_sum)
     partial_sum = jnp.stack(outs, axis=1).astype(jnp.bfloat16)

time: 347 us -> 324 us (0.934)
  waiting for transfers between devices: 204 us -> 192 us
  matrix products: 55.1 us -> 46.2 us
    psum x1, waiting for transfers between devices: 52.1 us -> 40.4 us  [lower_blocks_psum(): return lax.psum(packed, axis)]
    dot_general x2, matrix products: 25.6 us -> 16.7 us  [the longest x1 9.17 us: _mm(): lax.dot_general(a, b, dims, precision=precision, preferred_element_type=j...]
where the time goes in v7:
time: 324 us
  waiting for transfers between devices  192 us (59%)
  Pallas kernels  70.6 us (22%)
  matrix products  46.2 us (14%)
  between operations  13.9 us (4%)
    psum x1, waiting for transfers between devices, body(): sketch_rows = lax.psum(partial, 'rep')  83.6 us
    pallas_call x1, Pallas kernels, chol_inverse(): pl.pallas_call(_chol_inv_kernel, out_shape=jax.ShapeDtypeStruct((n, n), j...  70.6 us
    reduce_scatter x1, waiting for transfers between devices, body(): lax.psum_scatter(partial_sum, 'shard', scatter_dimension=0, tiled=True)  68.2 us
    psum x1, waiting for transfers between devices, lower_blocks_psum(): return lax.psum(packed, axis)  40.4 us
    dot_general x1, matrix products, body(): partial = jnp.dot(g, table, preferred_element_type=jnp.float32)  16.7 us
    dot_general x1, matrix products, body(): partial_sum = jnp.dot(basis_rows.T, g, preferred_element_type=jnp.float32)  12.8 us
    dot_general x1, matrix products, _mm(): lax.dot_general(a, b, dims, precision=precision, preferred_element_type=j...  9.17 us
    dot_general x1, matrix products, body(): jnp.dot(sketch_rows.T, sketch_rows, precision=lax.Precision.HIGH, preferr...  7.54 us
  transfers between devices with their start and end apart: 3, of which 3 were waited for; matrix products, arithmetic and copies ran while one was open for 0% of the time, Pallas kernels for 0%

profile of v7, /device:TPU:0, one launch (start us, length us, event | category | flops | bytes accessed | tf_op | source)
XLA Modules:
  0.0 324.1 jit_solution(1064736283045674976)
XLA Ops:
  6.5 0.0 all-reduce.3.cloned.1.call-start
  7.2 16.7 %fusion.27 = f32[2048,512]{0,1:T(8,128)} fusion(bf16[1,2048,3584]{2,1,0:T(8,128)(2,1)} %param.2, s32[]{:T(128)} %bitcast, s32[3584]{0:T(1024)S(1)} %add_multiply_fusion), kind=kOutput, calls=%fused_computation.24 | convolution fusion | flops 7540047872 | bytes 18888708 | tf_op jit(solution)/shard_map/dot_general | solution.py:113
  23.9 0.0 all-reduce.3.cloned.1.call-update
  23.9 0.0 all-reduce.5.cloned.1.call-start
  24.0 83.6 %all-reduce.3.cloned.1.call-done = f32[2048,512]{0,1:T(8,128)} async-done(((f32[2048,512]{0,1:T(8,128)}), f32[2048,512]{0,1:T(8,128)}) %all-reduce.3.cloned.1.call-update) | async-done | bytes 4194320 | tf_op jit(solution)/shard_map/psum | solution.py:114
  107.6 7.5 %fusion.49 = f32[512,512]{1,0:T(8,128)S(1)} fusion(f32[2048,512]{0,1:T(8,128)} %all-reduce.3.cloned.1.call-done), kind=kOutput, calls=%fused_computation.54 | convolution fusion | flops 3221225472 | bytes 5242880 | tf_op jit(solution)/shard_map/dot_general | solution.py:115
  115.4 0.0 copy-start
  115.4 0.8 copy-done
  116.2 0.0 all-reduce.5.cloned.1.call-update
  116.2 0.2 reduce-scatter.2.cloned.1.call-start
  116.5 40.4 %all-reduce.5.cloned.1.call-done.g_ref = f32[10,128,128]{2,1,0:T(8,128)} async-done(((f32[10,128,128]{2,1,0:T(8,128)}), f32[10,128,128]{2,1,0:T(8,128)}) %all-reduce.5.cloned.1.call-update) | async-done | bytes 655376 | tf_op jit(solution)/shard_map/psum | solution.py:103
  156.8 70.6 %shard_map.28 = f32[512,512]{1,0:T(8,128)} custom-call(f32[10,128,128]{2,1,0:T(8,128)} %all-reduce.5.cloned.1.call-done.g_ref), custom_call_target="tpu_custom_call" | custom-call | tf_op jit(solution)/shard_map/pallas_call | solution.py:71
  227.4 9.2 %convolution_convert_fusion = bf16[2048,512]{1,0:T(8,128)(2,1)S(1)} fusion(f32[2048,512]{0,1:T(8,128)} %all-reduce.3.cloned.1.call-done, f32[512,512]{1,0:T(8,128)} %shard_map.28), kind=kOutput, calls=%fused_computation.25 | convolution fusion | flops 3222274048 | bytes 7340032 | tf_op jit(solution)/shard_map/dot_general | solution.py:14
  236.6 12.8 %fusion.13 = bf16[512,1,3584]{2,0,1:T(8,128)(2,1)} fusion(bf16[2048,512]{1,0:T(8,128)(2,1)S(1)} %convolution_convert_fusion, bf16[1,2048,3584]{2,1,0:T(8,128)(2,1)} %param.2), kind=kOutput, calls=%fused_computation.13 | convolution fusion | flops 7518027776 | bytes 20447232 | tf_op jit(solution)/shard_map/dot_general | solution.py:125
  249.3 0.0 reduce-scatter.2.cloned.1.call-update
  249.4 68.2 %reduce-scatter.2.cloned.1.call-done = bf16[128,1,3584]{2,0,1:T(8,128)(2,1)} async-done(((bf16[512,1,3584]{2,0,1:T(8,128)(2,1)}), bf16[128,1,3584]{2,0,1:T(8,128)(2,1)}) %reduce-scatter.2.cloned.1.call-update) | async-done | bytes 917520 | tf_op jit(solution)/shard_map/reduce_scatter | solution.py:128
  (11 shorter events, 0.1 us)
Async XLA Ops:
  6.5 101.1 %all-reduce.3.cloned.1.call-start = ((), (), s32[]{:S(2)}) async-start(), calls=%async_computation.1 | async-start | bytes 8388608 | tf_op jit(solution)/shard_map/psum | solution.py:114
  23.9 132.9 %all-reduce.5.cloned.1.call-start = ((), (), s32[]{:S(2)}) async-start(), calls=%async_computation.2 | async-start | bytes 1310720 | tf_op jit(solution)/shard_map/psum | solution.py:103
  115.4 0.8 copy-start
  116.2 201.4 %reduce-scatter.2.cloned.1.call-start = ((), (), s32[]{:S(2)}) async-start(), calls=%async_computation.3 | async-start | bytes 4587520 | tf_op jit(solution)/shard_map/reduce_scatter | solution.py:128
Sparse Core Ops, SparseCore 0:
  24.1 83.5 all-reduce.2
  116.3 40.4 all-reduce.4
  249.5 68.0 reduce-scatter.1

commit v8 on v7

--- a/solution.py
+++ b/solution.py
@@ -45,13 +45,14 @@
             left = aug[:, :b]
             col = jnp.sum(jnp.where(bcol == k, left, 0.0), axis=1, keepdims=True)
             diag = jnp.sum(jnp.where(sub == k, col, 0.0), axis=0, keepdims=True)
-            inv = 1.0 / jnp.sqrt(diag)
+            inv = lax.rsqrt(diag)
+            inv = inv * (1.5 - 0.5 * diag * inv * inv)
             lrow = row * inv
             strict = jnp.where(sub > k, col * inv, 0.0)
             upd = aug - strict * lrow
             return jnp.where((arow == k) & (acol >= b), lrow, upd)
 
-        aug = lax.fori_loop(0, b, step, aug, unroll=4)
+        aug = lax.fori_loop(0, b, step, aug, unroll=8)
         winv = aug[:, b:]
         newtop = _mm(winv, w_ref[lo:lo + b, :])
         w_ref[lo:lo + b, :] = newtop

time: 324 us -> 321 us (level)
  no operation moved by 1% of the time
where the time goes in v8:
time: 321 us
  waiting for transfers between devices  192 us (60%)
  Pallas kernels  67.5 us (21%)
  matrix products  46 us (14%)
  between operations  13.9 us (4%)
    psum x1, waiting for transfers between devices, body(): sketch_rows = lax.psum(partial, 'rep')  83.5 us
    reduce_scatter x1, waiting for transfers between devices, body(): lax.psum_scatter(partial_sum, 'shard', scatter_dimension=0, tiled=True)  68.2 us
    pallas_call x1, Pallas kernels, chol_inverse(): pl.pallas_call(_chol_inv_kernel, out_shape=jax.ShapeDtypeStruct((n, n), j...  67.5 us
    psum x1, waiting for transfers between devices, lower_blocks_psum(): return lax.psum(packed, axis)  40.5 us
    dot_general x1, matrix products, body(): partial = jnp.dot(g, table, preferred_element_type=jnp.float32)  16.7 us
    dot_general x1, matrix products, body(): partial_sum = jnp.dot(basis_rows.T, g, preferred_element_type=jnp.float32)  12.5 us
    dot_general x1, matrix products, _mm(): lax.dot_general(a, b, dims, precision=precision, preferred_element_type=j...  9.17 us
    dot_general x1, matrix products, body(): jnp.dot(sketch_rows.T, sketch_rows, precision=lax.Precision.HIGH, preferr...  7.54 us
  transfers between devices with their start and end apart: 3, of which 3 were waited for; matrix products, arithmetic and copies ran while one was open for 0% of the time, Pallas kernels for 0%

profile of v8, /device:TPU:0, one launch (start us, length us, event | category | flops | bytes accessed | tf_op | source)
XLA Modules:
  0.0 320.8 jit_solution(6922968579956819460)
XLA Ops:
  6.5 0.0 all-reduce.3.cloned.1.call-start
  7.2 16.7 %fusion.27 = f32[2048,512]{0,1:T(8,128)} fusion(bf16[1,2048,3584]{2,1,0:T(8,128)(2,1)} %param.2, s32[]{:T(128)} %bitcast, s32[3584]{0:T(1024)S(1)} %add_multiply_fusion), kind=kOutput, calls=%fused_computation.24 | convolution fusion | flops 7540047872 | bytes 18888708 | tf_op jit(solution)/shard_map/dot_general | solution.py:114
  23.9 0.0 all-reduce.3.cloned.1.call-update
  23.9 0.2 all-reduce.5.cloned.1.call-start
  24.2 83.5 %all-reduce.3.cloned.1.call-done = f32[2048,512]{0,1:T(8,128)} async-done(((f32[2048,512]{0,1:T(8,128)}), f32[2048,512]{0,1:T(8,128)}) %all-reduce.3.cloned.1.call-update) | async-done | bytes 4194320 | tf_op jit(solution)/shard_map/psum | solution.py:115
  107.6 7.5 %fusion.49 = f32[512,512]{1,0:T(8,128)S(1)} fusion(f32[2048,512]{0,1:T(8,128)} %all-reduce.3.cloned.1.call-done), kind=kOutput, calls=%fused_computation.54 | convolution fusion | flops 3221225472 | bytes 5242880 | tf_op jit(solution)/shard_map/dot_general | solution.py:116
  115.4 0.0 copy-start
  115.4 0.8 copy-done
  116.2 0.0 all-reduce.5.cloned.1.call-update
  116.2 0.0 reduce-scatter.2.cloned.1.call-start
  116.3 40.5 %all-reduce.5.cloned.1.call-done.g_ref = f32[10,128,128]{2,1,0:T(8,128)} async-done(((f32[10,128,128]{2,1,0:T(8,128)}), f32[10,128,128]{2,1,0:T(8,128)}) %all-reduce.5.cloned.1.call-update) | async-done | bytes 655376 | tf_op jit(solution)/shard_map/psum | solution.py:104
  156.8 67.5 %shard_map.28 = f32[512,512]{1,0:T(8,128)} custom-call(f32[10,128,128]{2,1,0:T(8,128)} %all-reduce.5.cloned.1.call-done.g_ref), custom_call_target="tpu_custom_call" | custom-call | tf_op jit(solution)/shard_map/pallas_call | solution.py:72
  224.3 9.2 %convolution_convert_fusion = bf16[2048,512]{1,0:T(8,128)(2,1)S(1)} fusion(f32[2048,512]{0,1:T(8,128)} %all-reduce.3.cloned.1.call-done, f32[512,512]{1,0:T(8,128)} %shard_map.28), kind=kOutput, calls=%fused_computation.25 | convolution fusion | flops 3222274048 | bytes 7340032 | tf_op jit(solution)/shard_map/dot_general | solution.py:14
  233.4 12.5 %fusion.13 = bf16[512,1,3584]{2,0,1:T(8,128)(2,1)} fusion(bf16[2048,512]{1,0:T(8,128)(2,1)S(1)} %convolution_convert_fusion, bf16[1,2048,3584]{2,1,0:T(8,128)(2,1)} %param.2), kind=kOutput, calls=%fused_computation.13 | convolution fusion | flops 7518027776 | bytes 20447232 | tf_op jit(solution)/shard_map/dot_general | solution.py:126
  246.0 0.0 reduce-scatter.2.cloned.1.call-update
  246.0 68.2 %reduce-scatter.2.cloned.1.call-done = bf16[128,1,3584]{2,0,1:T(8,128)(2,1)} async-done(((bf16[512,1,3584]{2,0,1:T(8,128)(2,1)}), bf16[128,1,3584]{2,0,1:T(8,128)(2,1)}) %reduce-scatter.2.cloned.1.call-update) | async-done | bytes 917520 | tf_op jit(solution)/shard_map/reduce_scatter | solution.py:129
  (11 shorter events, 0.1 us)
Async XLA Ops:
  6.5 101.1 %all-reduce.3.cloned.1.call-start = ((), (), s32[]{:S(2)}) async-start(), calls=%async_computation.1 | async-start | bytes 8388608 | tf_op jit(solution)/shard_map/psum | solution.py:115
  23.9 132.9 %all-reduce.5.cloned.1.call-start = ((), (), s32[]{:S(2)}) async-start(), calls=%async_computation.2 | async-start | bytes 1310720 | tf_op jit(solution)/shard_map/psum | solution.py:104
  115.4 0.8 copy-start
  116.2 198.0 %reduce-scatter.2.cloned.1.call-start = ((), (), s32[]{:S(2)}) async-start(), calls=%async_computation.3 | async-start | bytes 4587520 | tf_op jit(solution)/shard_map/reduce_scatter | solution.py:129
Sparse Core Ops, SparseCore 0:
  24.1 83.5 all-reduce.2
  116.3 40.4 all-reduce.4
  246.1 68.0 reduce-scatter.1

commit v9 on v8

--- a/solution.py
+++ b/solution.py
@@ -112,7 +112,10 @@
         table = sketch_table(seeds[m:m + 1], col0, width, RANK)[0]
         g = grads[m]
         partial = jnp.dot(g, table, preferred_element_type=jnp.float32)
-        sketch_rows = lax.psum(partial, "rep")
+        sketch_rows = lax.all_gather(
+            lax.psum_scatter(partial, "rep", scatter_dimension=0, tiled=True),
+            "rep", axis=0, tiled=True,
+        )
         local_gram = jnp.dot(
             sketch_rows.T, sketch_rows,
             precision=lax.Precision.HIGH,

time: 321 us -> 331 us (1.031)
  waiting for transfers between devices: 192 us -> 202 us
    psum x1 -> x0, waiting for transfers between devices: 83.5 us -> none  [body(): sketch_rows = lax.psum(partial, 'rep')]
    reduce_scatter x0 -> x1, waiting for transfers between devices: none -> 53.9 us  [body(): lax.psum_scatter(partial, 'rep', scatter_dimension=0, tiled=True)]
    all_gather x0 -> x1, waiting for transfers between devices: none -> 39 us  [body(): lax.all_gather(lax.psum_scatter(partial, 'rep', scatter_dimension=0, tile...]
  transfers between devices with their start and end apart: 3 -> 4, of which waited for: 3 -> 4; matrix products, arithmetic and copies ran while one was open for 0% -> 0% of each run, Pallas kernels for 0% -> 0%
where the time goes in v9:
time: 331 us; the launch traced here: 330 us
  waiting for transfers between devices  202 us (61%)
  Pallas kernels  67.5 us (20%)
  matrix products  45.9 us (14%)
  between operations  13.9 us (4%)
    reduce_scatter x1, waiting for transfers between devices, body(): lax.psum_scatter(partial_sum, 'shard', scatter_dimension=0, tiled=True)  68.2 us
    pallas_call x1, Pallas kernels, chol_inverse(): pl.pallas_call(_chol_inv_kernel, out_shape=jax.ShapeDtypeStruct((n, n), j...  67.5 us
    reduce_scatter x1, waiting for transfers between devices, body(): lax.psum_scatter(partial, 'rep', scatter_dimension=0, tiled=True)  53.9 us
    psum x1, waiting for transfers between devices, lower_blocks_psum(): return lax.psum(packed, axis)  40.6 us
    all_gather x1, waiting for transfers between devices, body(): lax.all_gather(lax.psum_scatter(partial, 'rep', scatter_dimension=0, tile...  39 us
    dot_general x1, matrix products, body(): partial = jnp.dot(g, table, preferred_element_type=jnp.float32)  16.7 us
    dot_general x1, matrix products, body(): partial_sum = jnp.dot(basis_rows.T, g, preferred_element_type=jnp.float32)  12.5 us
    dot_general x1, matrix products, _mm(): lax.dot_general(a, b, dims, precision=precision, preferred_element_type=j...  9.17 us
  transfers between devices with their start and end apart: 4, of which 4 were waited for; matrix products, arithmetic and copies ran while one was open for 0% of the time, Pallas kernels for 0%

profile of v9, /device:TPU:0, one launch (start us, length us, event | category | flops | bytes accessed | tf_op | source)
XLA Modules:
  0.0 330.3 jit_solution(13864600763710721778)
XLA Ops:
  6.5 0.0 reduce-scatter.3.cloned.1.call-start
  7.2 16.7 %fusion.27 = f32[2048,512]{0,1:T(8,128)} fusion(bf16[1,2048,3584]{2,1,0:T(8,128)(2,1)} %param.2, s32[]{:T(128)} %bitcast, s32[3584]{0:T(1024)S(1)} %add_multiply_fusion), kind=kOutput, calls=%fused_computation.24 | convolution fusion | flops 7540047872 | bytes 18888708 | tf_op jit(solution)/shard_map/dot_general | solution.py:114
  23.9 0.0 reduce-scatter.3.cloned.1.call-update
  23.9 0.0 all-gather.2.cloned.1.call-start
  24.0 53.9 %reduce-scatter.3.cloned.1.call-done = f32[256,512]{0,1:T(8,128)} async-done(((f32[2048,512]{0,1:T(8,128)}), f32[256,512]{0,1:T(8,128)}) %reduce-scatter.3.cloned.1.call-update) | async-done | bytes 524304 | tf_op jit(solution)/shard_map/reduce_scatter | solution.py:116
  77.8 0.0 all-gather.2.cloned.1.call-update
  77.9 0.2 all-reduce.2.cloned.1.call-start
  78.1 39.0 %all-gather.2.cloned.1.call-done = f32[2048,512]{0,1:T(8,128)} async-done(((f32[256,512]{0,1:T(8,128)}), f32[2048,512]{0,1:T(8,128)}) %all-gather.2.cloned.1.call-update) | async-done | bytes 4194320 | tf_op jit(solution)/shard_map/all_gather | solution.py:115
  117.1 7.5 %fusion.49 = f32[512,512]{1,0:T(8,128)S(1)} fusion(f32[2048,512]{0,1:T(8,128)} %all-gather.2.cloned.1.call-done), kind=kOutput, calls=%fused_computation.54 | convolution fusion | flops 3221225472 | bytes 5242880 | tf_op jit(solution)/shard_map/dot_general | solution.py:119
  124.8 0.0 copy-start
  124.8 0.8 copy-done
  125.7 0.0 all-reduce.2.cloned.1.call-update
  125.7 0.0 reduce-scatter.5.cloned.1.call-start
  125.7 40.6 %all-reduce.2.cloned.1.call-done.g_ref = f32[10,128,128]{2,1,0:T(8,128)} async-done(((f32[10,128,128]{2,1,0:T(8,128)}), f32[10,128,128]{2,1,0:T(8,128)}) %all-reduce.2.cloned.1.call-update) | async-done | bytes 655376 | tf_op jit(solution)/shard_map/psum | solution.py:104
  166.4 67.5 %shard_map.28 = f32[512,512]{1,0:T(8,128)} custom-call(f32[10,128,128]{2,1,0:T(8,128)} %all-reduce.2.cloned.1.call-done.g_ref), custom_call_target="tpu_custom_call" | custom-call | tf_op jit(solution)/shard_map/pallas_call | solution.py:72
  233.8 9.2 %convolution_convert_fusion = bf16[2048,512]{1,0:T(8,128)(2,1)S(1)} fusion(f32[2048,512]{0,1:T(8,128)} %all-gather.2.cloned.1.call-done, f32[512,512]{1,0:T(8,128)} %shard_map.28), kind=kOutput, calls=%fused_computation.25 | convolution fusion | flops 3222274048 | bytes 7340032 | tf_op jit(solution)/shard_map/dot_general | solution.py:14
  243.0 12.5 %fusion.13 = bf16[512,1,3584]{2,0,1:T(8,128)(2,1)} fusion(bf16[2048,512]{1,0:T(8,128)(2,1)S(1)} %convolution_convert_fusion, bf16[1,2048,3584]{2,1,0:T(8,128)(2,1)} %param.2), kind=kOutput, calls=%fused_computation.13 | convolution fusion | flops 7518027776 | bytes 20447232 | tf_op jit(solution)/shard_map/dot_general | solution.py:129
  255.5 0.0 reduce-scatter.5.cloned.1.call-update
  255.5 68.2 %reduce-scatter.5.cloned.1.call-done = bf16[128,1,3584]{2,0,1:T(8,128)(2,1)} async-done(((bf16[512,1,3584]{2,0,1:T(8,128)(2,1)}), bf16[128,1,3584]{2,0,1:T(8,128)(2,1)}) %reduce-scatter.5.cloned.1.call-update) | async-done | bytes 917520 | tf_op jit(solution)/shard_map/reduce_scatter | solution.py:132
  (11 shorter events, 0.1 us)
Async XLA Ops:
  6.5 71.3 %reduce-scatter.3.cloned.1.call-start = ((), (), s32[]{:S(2)}) async-start(), calls=%async_computation.2 | async-start | bytes 4718592 | tf_op jit(solution)/shard_map/reduce_scatter | solution.py:116
  23.9 93.2 %all-gather.2.cloned.1.call-start = ((), (), s32[]{:S(2)}) async-start(), calls=%async_computation.3 | async-start | bytes 4718592 | tf_op jit(solution)/shard_map/all_gather | solution.py:115
  77.9 88.5 %all-reduce.2.cloned.1.call-start = ((), (), s32[]{:S(2)}) async-start(), calls=%async_computation.4 | async-start | bytes 1310720 | tf_op jit(solution)/shard_map/psum | solution.py:104
  124.8 0.8 copy-start
  125.7 198.1 %reduce-scatter.5.cloned.1.call-start = ((), (), s32[]{:S(2)}) async-start(), calls=%async_computation.5 | async-start | bytes 4587520 | tf_op jit(solution)/shard_map/reduce_scatter | solution.py:132
Sparse Core Ops, SparseCore 0:
  24.0 53.7 reduce-scatter.2
  79.7 37.3 all-gather.1
  125.8 40.5 all-reduce.1
  255.7 68.0 reduce-scatter.4

commit v10 on v7

--- a/solution.py
+++ b/solution.py
@@ -7,6 +7,7 @@
 
 RANK = 512
 BLOCK = 128
+STAGES = 4
 
 
 def _mm(a, b, trans_b=False, precision=lax.Precision.HIGHEST):
@@ -40,18 +41,31 @@
         blk = a_ref[_tri(p, p)]
         aug = jnp.where(acol < b, jnp.concatenate([blk, blk], axis=1), eye)
 
-        def step(k, aug):
-            row = jnp.sum(jnp.where(arow == k, aug, 0.0), axis=0, keepdims=True)
-            left = aug[:, :b]
-            col = jnp.sum(jnp.where(bcol == k, left, 0.0), axis=1, keepdims=True)
-            diag = jnp.sum(jnp.where(sub == k, col, 0.0), axis=0, keepdims=True)
-            inv = 1.0 / jnp.sqrt(diag)
-            lrow = row * inv
-            strict = jnp.where(sub > k, col * inv, 0.0)
-            upd = aug - strict * lrow
-            return jnp.where((arow == k) & (acol >= b), lrow, upd)
+        parts = []
+        for q in range(STAGES):
+            r0 = q * b // STAGES
+            arow_q = arow[r0:]
+            acol_q = acol[r0:]
+            sub_q = sub[r0:]
 
-        aug = lax.fori_loop(0, b, step, aug, unroll=4)
+            def step(k, low, arow_q=arow_q, acol_q=acol_q, sub_q=sub_q):
+                row = jnp.sum(jnp.where(arow_q == k, low, 0.0), axis=0, keepdims=True)
+                left = low[:, :b]
+                col = jnp.sum(
+                    jnp.where(bcol[:left.shape[0]] == k, left, 0.0), axis=1, keepdims=True
+                )
+                diag = jnp.sum(jnp.where(sub_q == k, col, 0.0), axis=0, keepdims=True)
+                inv = lax.rsqrt(diag)
+                inv = inv * (1.5 - 0.5 * diag * inv * inv)
+                lrow = row * inv
+                strict = jnp.where(sub_q > k, col * inv, 0.0)
+                upd = low - strict * lrow
+                return jnp.where((arow_q == k) & (acol_q >= b), lrow, upd)
+
+            low = lax.fori_loop(r0, r0 + b // STAGES, step, aug[r0:], unroll=4)
+            r1 = (q + 1) * b // STAGES
+            parts.append(low[:r1 - r0])
+            aug = jnp.concatenate(parts + ([low[r1 - r0:]] if q + 1 < STAGES else []), axis=0)
         winv = aug[:, b:]
         newtop = _mm(winv, w_ref[lo:lo + b, :])
         w_ref[lo:lo + b, :] = newtop

time: 324 us -> 318 us (0.981)
  Pallas kernels: 70.6 us -> 64.2 us
    pallas_call x1, Pallas kernels: 70.6 us -> 64.2 us  [chol_inverse(): pl.pallas_call(_chol_inv_kernel, out_shape=jax.ShapeDtypeStruct((n, n), j...]
where the time goes in v10:
time: 318 us
  waiting for transfers between devices  192 us (60%)
  Pallas kernels  64.2 us (20%)
  matrix products  46 us (14%)
  between operations  13.9 us (4%)
    psum x1, waiting for transfers between devices, body(): sketch_rows = lax.psum(partial, 'rep')  83.5 us
    reduce_scatter x1, waiting for transfers between devices, body(): lax.psum_scatter(partial_sum, 'shard', scatter_dimension=0, tiled=True)  68.2 us
    pallas_call x1, Pallas kernels, chol_inverse(): pl.pallas_call(_chol_inv_kernel, out_shape=jax.ShapeDtypeStruct((n, n), j...  64.2 us
    psum x1, waiting for transfers between devices, lower_blocks_psum(): return lax.psum(packed, axis)  40.5 us
    dot_general x1, matrix products, body(): partial = jnp.dot(g, table, preferred_element_type=jnp.float32)  16.7 us
    dot_general x1, matrix products, body(): partial_sum = jnp.dot(basis_rows.T, g, preferred_element_type=jnp.float32)  12.5 us
    dot_general x1, matrix products, _mm(): lax.dot_general(a, b, dims, precision=precision, preferred_element_type=j...  9.17 us
    dot_general x1, matrix products, body(): jnp.dot(sketch_rows.T, sketch_rows, precision=lax.Precision.HIGH, preferr...  7.54 us
  transfers between devices with their start and end apart: 3, of which 3 were waited for; matrix products, arithmetic and copies ran while one was open for 0% of the time, Pallas kernels for 0%

profile of v10, /device:TPU:0, one launch (start us, length us, event | category | flops | bytes accessed | tf_op | source)
XLA Modules:
  0.0 317.5 jit_solution(2553952159194906070)
XLA Ops:
  6.5 0.0 all-reduce.3.cloned.1.call-start
  7.2 16.7 %fusion.27 = f32[2048,512]{0,1:T(8,128)} fusion(bf16[1,2048,3584]{2,1,0:T(8,128)(2,1)} %param.2, s32[]{:T(128)} %bitcast, s32[3584]{0:T(1024)S(1)} %add_multiply_fusion), kind=kOutput, calls=%fused_computation.24 | convolution fusion | flops 7540047872 | bytes 18888708 | tf_op jit(solution)/shard_map/dot_general | solution.py:127
  23.9 0.0 all-reduce.3.cloned.1.call-update
  23.9 0.2 all-reduce.5.cloned.1.call-start
  24.2 83.5 %all-reduce.3.cloned.1.call-done = f32[2048,512]{0,1:T(8,128)} async-done(((f32[2048,512]{0,1:T(8,128)}), f32[2048,512]{0,1:T(8,128)}) %all-reduce.3.cloned.1.call-update) | async-done | bytes 4194320 | tf_op jit(solution)/shard_map/psum | solution.py:128
  107.6 7.5 %fusion.49 = f32[512,512]{1,0:T(8,128)S(1)} fusion(f32[2048,512]{0,1:T(8,128)} %all-reduce.3.cloned.1.call-done), kind=kOutput, calls=%fused_computation.54 | convolution fusion | flops 3221225472 | bytes 5242880 | tf_op jit(solution)/shard_map/dot_general | solution.py:129
  115.4 0.0 copy-start
  115.4 0.8 copy-done
  116.2 0.0 all-reduce.5.cloned.1.call-update
  116.2 0.0 reduce-scatter.2.cloned.1.call-start
  116.3 40.5 %all-reduce.5.cloned.1.call-done.g_ref = f32[10,128,128]{2,1,0:T(8,128)} async-done(((f32[10,128,128]{2,1,0:T(8,128)}), f32[10,128,128]{2,1,0:T(8,128)}) %all-reduce.5.cloned.1.call-update) | async-done | bytes 655376 | tf_op jit(solution)/shard_map/psum | solution.py:117
  156.8 64.2 %shard_map.28 = f32[512,512]{1,0:T(8,128)} custom-call(f32[10,128,128]{2,1,0:T(8,128)} %all-reduce.5.cloned.1.call-done.g_ref), custom_call_target="tpu_custom_call" | custom-call | tf_op jit(solution)/shard_map/pallas_call | solution.py:85
  221.0 9.2 %convolution_convert_fusion = bf16[2048,512]{1,0:T(8,128)(2,1)S(1)} fusion(f32[2048,512]{0,1:T(8,128)} %all-reduce.3.cloned.1.call-done, f32[512,512]{1,0:T(8,128)} %shard_map.28), kind=kOutput, calls=%fused_computation.25 | convolution fusion | flops 3222274048 | bytes 7340032 | tf_op jit(solution)/shard_map/dot_general | solution.py:15
  230.2 12.5 %fusion.13 = bf16[512,1,3584]{2,0,1:T(8,128)(2,1)} fusion(bf16[2048,512]{1,0:T(8,128)(2,1)S(1)} %convolution_convert_fusion, bf16[1,2048,3584]{2,1,0:T(8,128)(2,1)} %param.2), kind=kOutput, calls=%fused_computation.13 | convolution fusion | flops 7518027776 | bytes 20447232 | tf_op jit(solution)/shard_map/dot_general | solution.py:139
  242.7 0.0 reduce-scatter.2.cloned.1.call-update
  242.8 68.2 %reduce-scatter.2.cloned.1.call-done = bf16[128,1,3584]{2,0,1:T(8,128)(2,1)} async-done(((bf16[512,1,3584]{2,0,1:T(8,128)(2,1)}), bf16[128,1,3584]{2,0,1:T(8,128)(2,1)}) %reduce-scatter.2.cloned.1.call-update) | async-done | bytes 917520 | tf_op jit(solution)/shard_map/reduce_scatter | solution.py:142
  (11 shorter events, 0.1 us)
Async XLA Ops:
  6.5 101.1 %all-reduce.3.cloned.1.call-start = ((), (), s32[]{:S(2)}) async-start(), calls=%async_computation.1 | async-start | bytes 8388608 | tf_op jit(solution)/shard_map/psum | solution.py:128
  23.9 132.9 %all-reduce.5.cloned.1.call-start = ((), (), s32[]{:S(2)}) async-start(), calls=%async_computation.2 | async-start | bytes 1310720 | tf_op jit(solution)/shard_map/psum | solution.py:117
  115.4 0.8 copy-start
  116.2 194.8 %reduce-scatter.2.cloned.1.call-start = ((), (), s32[]{:S(2)}) async-start(), calls=%async_computation.3 | async-start | bytes 4587520 | tf_op jit(solution)/shard_map/reduce_scatter | solution.py:142
Sparse Core Ops, SparseCore 0:
  24.1 83.5 all-reduce.2
  116.3 40.4 all-reduce.4
  242.9 68.0 reduce-scatter.1

commit v11 on v10

--- a/solution.py
+++ b/solution.py
@@ -62,7 +62,7 @@
                 upd = low - strict * lrow
                 return jnp.where((arow_q == k) & (acol_q >= b), lrow, upd)
 
-            low = lax.fori_loop(r0, r0 + b // STAGES, step, aug[r0:], unroll=4)
+            low = lax.fori_loop(r0, r0 + b // STAGES, step, aug[r0:], unroll=2)
             r1 = (q + 1) * b // STAGES
             parts.append(low[:r1 - r0])
             aug = jnp.concatenate(parts + ([low[r1 - r0:]] if q + 1 < STAGES else []), axis=0)
@@ -128,14 +128,12 @@
         sketch_rows = lax.psum(partial, "rep")
         local_gram = jnp.dot(
             sketch_rows.T, sketch_rows,
-            precision=lax.Precision.HIGH,
+            precision=lax.Precision.HIGHEST,
             preferred_element_type=jnp.float32,
         )
         gram = lower_blocks_psum(local_gram, "shard")
         inverse = chol_inverse(gram)
-        basis_rows = _mm(
-            sketch_rows, inverse, trans_b=True, precision=lax.Precision.HIGH
-        ).astype(jnp.bfloat16)
+        basis_rows = _mm(sketch_rows, inverse, trans_b=True).astype(jnp.bfloat16)
         partial_sum = jnp.dot(basis_rows.T, g, preferred_element_type=jnp.float32)
         outs.append(partial_sum)
     partial_sum = jnp.stack(outs, axis=1).astype(jnp.bfloat16)

time: 318 us -> 327 us (1.028)
  matrix products: 46 us -> 54 us
    dot_general x1, matrix products: 9.17 us -> 15.2 us  [_mm(): lax.dot_general(a, b, dims, precision=precision, preferred_element_type=j...]
where the time goes in v11:
time: 327 us
  waiting for transfers between devices  192 us (59%)
  Pallas kernels  65.4 us (20%)
  matrix products  54 us (17%)
  between operations  13.9 us (4%)
    psum x1, waiting for transfers between devices, body(): sketch_rows = lax.psum(partial, 'rep')  83.5 us
    reduce_scatter x1, waiting for transfers between devices, body(): lax.psum_scatter(partial_sum, 'shard', scatter_dimension=0, tiled=True)  68.2 us
    pallas_call x1, Pallas kernels, chol_inverse(): pl.pallas_call(_chol_inv_kernel, out_shape=jax.ShapeDtypeStruct((n, n), j...  65.4 us
    psum x1, waiting for transfers between devices, lower_blocks_psum(): return lax.psum(packed, axis)  40.5 us
    dot_general x1, matrix products, body(): partial = jnp.dot(g, table, preferred_element_type=jnp.float32)  16.7 us
    dot_general x1, matrix products, _mm(): lax.dot_general(a, b, dims, precision=precision, preferred_element_type=j...  15.2 us
    dot_general x1, matrix products, body(): partial_sum = jnp.dot(basis_rows.T, g, preferred_element_type=jnp.float32)  12.8 us
    dot_general x1, matrix products, body(): jnp.dot(sketch_rows.T, sketch_rows, precision=lax.Precision.HIGHEST, pref...  9.34 us
  transfers between devices with their start and end apart: 3, of which 3 were waited for; matrix products, arithmetic and copies ran while one was open for 0% of the time, Pallas kernels for 0%

profile of v11, /device:TPU:0, one launch (start us, length us, event | category | flops | bytes accessed | tf_op | source)
XLA Modules:
  0.0 326.8 jit_solution(2148399347342884542)
XLA Ops:
  6.5 0.0 all-reduce.3.cloned.1.call-start
  7.2 16.7 %fusion.27 = f32[2048,512]{0,1:T(8,128)} fusion(bf16[1,2048,3584]{2,1,0:T(8,128)(2,1)} %param.2, s32[]{:T(128)} %bitcast, s32[3584]{0:T(1024)S(1)} %add_multiply_fusion), kind=kOutput, calls=%fused_computation.24 | convolution fusion | flops 7540047872 | bytes 18888708 | tf_op jit(solution)/shard_map/dot_general | solution.py:127
  23.9 0.0 all-reduce.3.cloned.1.call-update
  23.9 0.2 all-reduce.5.cloned.1.call-start
  24.2 83.5 %all-reduce.3.cloned.1.call-done = f32[2048,512]{0,1:T(8,128)} async-done(((f32[2048,512]{0,1:T(8,128)}), f32[2048,512]{0,1:T(8,128)}) %all-reduce.3.cloned.1.call-update) | async-done | bytes 4194320 | tf_op jit(solution)/shard_map/psum | solution.py:128
  107.6 9.3 %fusion.49 = f32[512,512]{1,0:T(8,128)S(1)} fusion(f32[2048,512]{0,1:T(8,128)} %all-reduce.3.cloned.1.call-done), kind=kOutput, calls=%fused_computation.54 | convolution fusion | flops 6442450944 | bytes 5242880 | tf_op jit(solution)/shard_map/dot_general | solution.py:129
  117.2 0.0 copy-start
  117.2 0.8 copy-done
  118.0 0.0 all-reduce.5.cloned.1.call-update
  118.0 0.0 reduce-scatter.2.cloned.1.call-start
  118.1 40.5 %all-reduce.5.cloned.1.call-done.g_ref = f32[10,128,128]{2,1,0:T(8,128)} async-done(((f32[10,128,128]{2,1,0:T(8,128)}), f32[10,128,128]{2,1,0:T(8,128)}) %all-reduce.5.cloned.1.call-update) | async-done | bytes 655376 | tf_op jit(solution)/shard_map/psum | solution.py:117
  158.6 65.4 %shard_map.28 = f32[512,512]{1,0:T(8,128)} custom-call(f32[10,128,128]{2,1,0:T(8,128)} %all-reduce.5.cloned.1.call-done.g_ref), custom_call_target="tpu_custom_call" | custom-call | tf_op jit(solution)/shard_map/pallas_call | solution.py:85
  224.1 15.2 %convolution_convert_fusion = bf16[2048,512]{1,0:T(8,128)(2,1)S(1)} fusion(f32[2048,512]{0,1:T(8,128)} %all-reduce.3.cloned.1.call-done, f32[512,512]{1,0:T(8,128)} %shard_map.28), kind=kOutput, calls=%fused_computation.25 | convolution fusion | flops 6443499520 | bytes 7340032 | tf_op jit(solution)/shard_map/dot_general | solution.py:15
  239.3 12.8 %fusion.13 = bf16[512,1,3584]{2,0,1:T(8,128)(2,1)} fusion(bf16[2048,512]{1,0:T(8,128)(2,1)S(1)} %convolution_convert_fusion, bf16[1,2048,3584]{2,1,0:T(8,128)(2,1)} %param.2), kind=kOutput, calls=%fused_computation.13 | convolution fusion | flops 7518027776 | bytes 20447232 | tf_op jit(solution)/shard_map/dot_general | solution.py:137
  252.0 0.0 reduce-scatter.2.cloned.1.call-update
  252.0 68.2 %reduce-scatter.2.cloned.1.call-done = bf16[128,1,3584]{2,0,1:T(8,128)(2,1)} async-done(((bf16[512,1,3584]{2,0,1:T(8,128)(2,1)}), bf16[128,1,3584]{2,0,1:T(8,128)(2,1)}) %reduce-scatter.2.cloned.1.call-update) | async-done | bytes 917520 | tf_op jit(solution)/shard_map/reduce_scatter | solution.py:140
  (11 shorter events, 0.1 us)
Async XLA Ops:
  6.5 101.1 %all-reduce.3.cloned.1.call-start = ((), (), s32[]{:S(2)}) async-start(), calls=%async_computation.1 | async-start | bytes 8388608 | tf_op jit(solution)/shard_map/psum | solution.py:128
  23.9 134.7 %all-reduce.5.cloned.1.call-start = ((), (), s32[]{:S(2)}) async-start(), calls=%async_computation.2 | async-start | bytes 1310720 | tf_op jit(solution)/shard_map/psum | solution.py:117
  117.2 0.8 copy-start
  118.0 202.3 %reduce-scatter.2.cloned.1.call-start = ((), (), s32[]{:S(2)}) async-start(), calls=%async_computation.3 | async-start | bytes 4587520 | tf_op jit(solution)/shard_map/reduce_scatter | solution.py:140
Sparse Core Ops, SparseCore 0:
  24.1 83.5 all-reduce.2
  118.1 40.4 all-reduce.4
  252.2 68.0 reduce-scatter.1

commit v12 on v11

--- a/solution.py
+++ b/solution.py
@@ -7,7 +7,7 @@
 
 RANK = 512
 BLOCK = 128
-STAGES = 4
+STAGES = 8
 
 
 def _mm(a, b, trans_b=False, precision=lax.Precision.HIGHEST):
@@ -62,7 +62,7 @@
                 upd = low - strict * lrow
                 return jnp.where((arow_q == k) & (acol_q >= b), lrow, upd)
 
-            low = lax.fori_loop(r0, r0 + b // STAGES, step, aug[r0:], unroll=2)
+            low = lax.fori_loop(r0, r0 + b // STAGES, step, aug[r0:], unroll=1)
             r1 = (q + 1) * b // STAGES
             parts.append(low[:r1 - r0])
             aug = jnp.concatenate(parts + ([low[r1 - r0:]] if q + 1 < STAGES else []), axis=0)

time: 327 us -> 329 us (level)
  no operation moved by 1% of the time
where the time goes in v12:
time: 329 us; the launch traced here: 328 us
  waiting for transfers between devices  192 us (58%)
  Pallas kernels  66.9 us (20%)
  matrix products  54 us (16%)
  between operations  13.9 us (4%)
    psum x1, waiting for transfers between devices, body(): sketch_rows = lax.psum(partial, 'rep')  83.5 us
    reduce_scatter x1, waiting for transfers between devices, body(): lax.psum_scatter(partial_sum, 'shard', scatter_dimension=0, tiled=True)  68.2 us
    pallas_call x1, Pallas kernels, chol_inverse(): pl.pallas_call(_chol_inv_kernel, out_shape=jax.ShapeDtypeStruct((n, n), j...  66.9 us
    psum x1, waiting for transfers between devices, lower_blocks_psum(): return lax.psum(packed, axis)  40.5 us
    dot_general x1, matrix products, body(): partial = jnp.dot(g, table, preferred_element_type=jnp.float32)  16.7 us
    dot_general x1, matrix products, _mm(): lax.dot_general(a, b, dims, precision=precision, preferred_element_type=j...  15.2 us
    dot_general x1, matrix products, body(): partial_sum = jnp.dot(basis_rows.T, g, preferred_element_type=jnp.float32)  12.8 us
    dot_general x1, matrix products, body(): jnp.dot(sketch_rows.T, sketch_rows, precision=lax.Precision.HIGHEST, pref...  9.34 us
  transfers between devices with their start and end apart: 3, of which 3 were waited for; matrix products, arithmetic and copies ran while one was open for 0% of the time, Pallas kernels for 0%

profile of v12, /device:TPU:0, one launch (start us, length us, event | category | flops | bytes accessed | tf_op | source)
XLA Modules:
  0.0 328.3 jit_solution(1034522943306884742)
XLA Ops:
  6.5 0.0 all-reduce.3.cloned.1.call-start
  7.2 16.7 %fusion.27 = f32[2048,512]{0,1:T(8,128)} fusion(bf16[1,2048,3584]{2,1,0:T(8,128)(2,1)} %param.2, s32[]{:T(128)} %bitcast, s32[3584]{0:T(1024)S(1)} %add_multiply_fusion), kind=kOutput, calls=%fused_computation.24 | convolution fusion | flops 7540047872 | bytes 18888708 | tf_op jit(solution)/shard_map/dot_general | solution.py:127
  23.9 0.0 all-reduce.3.cloned.1.call-update
  23.9 0.2 all-reduce.5.cloned.1.call-start
  24.2 83.5 %all-reduce.3.cloned.1.call-done = f32[2048,512]{0,1:T(8,128)} async-done(((f32[2048,512]{0,1:T(8,128)}), f32[2048,512]{0,1:T(8,128)}) %all-reduce.3.cloned.1.call-update) | async-done | bytes 4194320 | tf_op jit(solution)/shard_map/psum | solution.py:128
  107.6 9.3 %fusion.49 = f32[512,512]{1,0:T(8,128)S(1)} fusion(f32[2048,512]{0,1:T(8,128)} %all-reduce.3.cloned.1.call-done), kind=kOutput, calls=%fused_computation.54 | convolution fusion | flops 6442450944 | bytes 5242880 | tf_op jit(solution)/shard_map/dot_general | solution.py:129
  117.2 0.0 copy-start
  117.2 0.8 copy-done
  118.0 0.0 all-reduce.5.cloned.1.call-update
  118.0 0.0 reduce-scatter.2.cloned.1.call-start
  118.1 40.5 %all-reduce.5.cloned.1.call-done.g_ref = f32[10,128,128]{2,1,0:T(8,128)} async-done(((f32[10,128,128]{2,1,0:T(8,128)}), f32[10,128,128]{2,1,0:T(8,128)}) %all-reduce.5.cloned.1.call-update) | async-done | bytes 655376 | tf_op jit(solution)/shard_map/psum | solution.py:117
  158.6 66.9 %shard_map.28 = f32[512,512]{1,0:T(8,128)} custom-call(f32[10,128,128]{2,1,0:T(8,128)} %all-reduce.5.cloned.1.call-done.g_ref), custom_call_target="tpu_custom_call" | custom-call | tf_op jit(solution)/shard_map/pallas_call | solution.py:85
  225.6 15.2 %convolution_convert_fusion = bf16[2048,512]{1,0:T(8,128)(2,1)S(1)} fusion(f32[2048,512]{0,1:T(8,128)} %all-reduce.3.cloned.1.call-done, f32[512,512]{1,0:T(8,128)} %shard_map.28), kind=kOutput, calls=%fused_computation.25 | convolution fusion | flops 6443499520 | bytes 7340032 | tf_op jit(solution)/shard_map/dot_general | solution.py:15
  240.8 12.8 %fusion.13 = bf16[512,1,3584]{2,0,1:T(8,128)(2,1)} fusion(bf16[2048,512]{1,0:T(8,128)(2,1)S(1)} %convolution_convert_fusion, bf16[1,2048,3584]{2,1,0:T(8,128)(2,1)} %param.2), kind=kOutput, calls=%fused_computation.13 | convolution fusion | flops 7518027776 | bytes 20447232 | tf_op jit(solution)/shard_map/dot_general | solution.py:137
  253.5 0.0 reduce-scatter.2.cloned.1.call-update
  253.5 68.2 %reduce-scatter.2.cloned.1.call-done = bf16[128,1,3584]{2,0,1:T(8,128)(2,1)} async-done(((bf16[512,1,3584]{2,0,1:T(8,128)(2,1)}), bf16[128,1,3584]{2,0,1:T(8,128)(2,1)}) %reduce-scatter.2.cloned.1.call-update) | async-done | bytes 917520 | tf_op jit(solution)/shard_map/reduce_scatter | solution.py:140
  (11 shorter events, 0.1 us)
Async XLA Ops:
  6.5 101.1 %all-reduce.3.cloned.1.call-start = ((), (), s32[]{:S(2)}) async-start(), calls=%async_computation.1 | async-start | bytes 8388608 | tf_op jit(solution)/shard_map/psum | solution.py:128
  23.9 134.7 %all-reduce.5.cloned.1.call-start = ((), (), s32[]{:S(2)}) async-start(), calls=%async_computation.2 | async-start | bytes 1310720 | tf_op jit(solution)/shard_map/psum | solution.py:117
  117.2 0.8 copy-start
  118.0 203.8 %reduce-scatter.2.cloned.1.call-start = ((), (), s32[]{:S(2)}) async-start(), calls=%async_computation.3 | async-start | bytes 4587520 | tf_op jit(solution)/shard_map/reduce_scatter | solution.py:140
Sparse Core Ops, SparseCore 0:
  24.1 83.5 all-reduce.2
  118.1 40.4 all-reduce.4
  253.7 68.0 reduce-scatter.1

commit v13 on v11

--- a/solution.py
+++ b/solution.py
@@ -67,13 +67,14 @@
             parts.append(low[:r1 - r0])
             aug = jnp.concatenate(parts + ([low[r1 - r0:]] if q + 1 < STAGES else []), axis=0)
         winv = aug[:, b:]
-        newtop = _mm(winv, w_ref[lo:lo + b, :])
-        w_ref[lo:lo + b, :] = newtop
+        hi = lo + b
+        newtop = _mm(winv, w_ref[lo:lo + b, :hi])
+        w_ref[lo:lo + b, :hi] = newtop
         panels = {i: _mm(a_ref[_tri(i, p)], winv, trans_b=True) for i in range(p + 1, nb)}
         for i in range(p + 1, nb):
             for j in range(p + 1, i + 1):
                 a_ref[_tri(i, j)] = a_ref[_tri(i, j)] - _mm(panels[i], panels[j], trans_b=True)
-            w_ref[i * b:(i + 1) * b, :] = w_ref[i * b:(i + 1) * b, :] - _mm(panels[i], newtop)
+            w_ref[i * b:(i + 1) * b, :hi] = w_ref[i * b:(i + 1) * b, :hi] - _mm(panels[i], newtop)
 
 
 def chol_inverse(packed):

time: 327 us -> 326 us (level)
  no operation moved by 1% of the time
where the time goes in v13:
time: 326 us
  waiting for transfers between devices  192 us (59%)
  Pallas kernels  64.2 us (20%)
  matrix products  54 us (17%)
  between operations  13.9 us (4%)
    psum x1, waiting for transfers between devices, body(): sketch_rows = lax.psum(partial, 'rep')  83.5 us
    reduce_scatter x1, waiting for transfers between devices, body(): lax.psum_scatter(partial_sum, 'shard', scatter_dimension=0, tiled=True)  68.2 us
    pallas_call x1, Pallas kernels, chol_inverse(): pl.pallas_call(_chol_inv_kernel, out_shape=jax.ShapeDtypeStruct((n, n), j...  64.2 us
    psum x1, waiting for transfers between devices, lower_blocks_psum(): return lax.psum(packed, axis)  40.5 us
    dot_general x1, matrix products, body(): partial = jnp.dot(g, table, preferred_element_type=jnp.float32)  16.7 us
    dot_general x1, matrix products, _mm(): lax.dot_general(a, b, dims, precision=precision, preferred_element_type=j...  15.2 us
    dot_general x1, matrix products, body(): partial_sum = jnp.dot(basis_rows.T, g, preferred_element_type=jnp.float32)  12.8 us
    dot_general x1, matrix products, body(): jnp.dot(sketch_rows.T, sketch_rows, precision=lax.Precision.HIGHEST, pref...  9.34 us
  transfers between devices with their start and end apart: 3, of which 3 were waited for; matrix products, arithmetic and copies ran while one was open for 0% of the time, Pallas kernels for 0%

profile of v13, /device:TPU:0, one launch (start us, length us, event | category | flops | bytes accessed | tf_op | source)
XLA Modules:
  0.0 325.6 jit_solution(5639898069927337786)
XLA Ops:
  6.5 0.0 all-reduce.3.cloned.1.call-start
  7.2 16.7 %fusion.27 = f32[2048,512]{0,1:T(8,128)} fusion(bf16[1,2048,3584]{2,1,0:T(8,128)(2,1)} %param.2, s32[]{:T(128)} %bitcast, s32[3584]{0:T(1024)S(1)} %add_multiply_fusion), kind=kOutput, calls=%fused_computation.24 | convolution fusion | flops 7540047872 | bytes 18888708 | tf_op jit(solution)/shard_map/dot_general | solution.py:128
  23.9 0.0 all-reduce.3.cloned.1.call-update
  23.9 0.2 all-reduce.5.cloned.1.call-start
  24.2 83.5 %all-reduce.3.cloned.1.call-done = f32[2048,512]{0,1:T(8,128)} async-done(((f32[2048,512]{0,1:T(8,128)}), f32[2048,512]{0,1:T(8,128)}) %all-reduce.3.cloned.1.call-update) | async-done | bytes 4194320 | tf_op jit(solution)/shard_map/psum | solution.py:129
  107.6 9.3 %fusion.49 = f32[512,512]{1,0:T(8,128)S(1)} fusion(f32[2048,512]{0,1:T(8,128)} %all-reduce.3.cloned.1.call-done), kind=kOutput, calls=%fused_computation.54 | convolution fusion | flops 6442450944 | bytes 5242880 | tf_op jit(solution)/shard_map/dot_general | solution.py:130
  117.2 0.0 copy-start
  117.2 0.8 copy-done
  118.0 0.0 all-reduce.5.cloned.1.call-update
  118.0 0.0 reduce-scatter.2.cloned.1.call-start
  118.1 40.5 %all-reduce.5.cloned.1.call-done.g_ref = f32[10,128,128]{2,1,0:T(8,128)} async-done(((f32[10,128,128]{2,1,0:T(8,128)}), f32[10,128,128]{2,1,0:T(8,128)}) %all-reduce.5.cloned.1.call-update) | async-done | bytes 655376 | tf_op jit(solution)/shard_map/psum | solution.py:118
  158.6 64.2 %shard_map.28 = f32[512,512]{1,0:T(8,128)} custom-call(f32[10,128,128]{2,1,0:T(8,128)} %all-reduce.5.cloned.1.call-done.g_ref), custom_call_target="tpu_custom_call" | custom-call | tf_op jit(solution)/shard_map/pallas_call | solution.py:86
  222.8 15.2 %convolution_convert_fusion = bf16[2048,512]{1,0:T(8,128)(2,1)S(1)} fusion(f32[2048,512]{0,1:T(8,128)} %all-reduce.3.cloned.1.call-done, f32[512,512]{1,0:T(8,128)} %shard_map.28), kind=kOutput, calls=%fused_computation.25 | convolution fusion | flops 6443499520 | bytes 7340032 | tf_op jit(solution)/shard_map/dot_general | solution.py:15
  238.0 12.8 %fusion.13 = bf16[512,1,3584]{2,0,1:T(8,128)(2,1)} fusion(bf16[2048,512]{1,0:T(8,128)(2,1)S(1)} %convolution_convert_fusion, bf16[1,2048,3584]{2,1,0:T(8,128)(2,1)} %param.2), kind=kOutput, calls=%fused_computation.13 | convolution fusion | flops 7518027776 | bytes 20447232 | tf_op jit(solution)/shard_map/dot_general | solution.py:138
  250.8 0.0 reduce-scatter.2.cloned.1.call-update
  250.8 68.2 %reduce-scatter.2.cloned.1.call-done = bf16[128,1,3584]{2,0,1:T(8,128)(2,1)} async-done(((bf16[512,1,3584]{2,0,1:T(8,128)(2,1)}), bf16[128,1,3584]{2,0,1:T(8,128)(2,1)}) %reduce-scatter.2.cloned.1.call-update) | async-done | bytes 917520 | tf_op jit(solution)/shard_map/reduce_scatter | solution.py:141
  (11 shorter events, 0.1 us)
Async XLA Ops:
  6.5 101.1 %all-reduce.3.cloned.1.call-start = ((), (), s32[]{:S(2)}) async-start(), calls=%async_computation.1 | async-start | bytes 8388608 | tf_op jit(solution)/shard_map/psum | solution.py:129
  23.9 134.7 %all-reduce.5.cloned.1.call-start = ((), (), s32[]{:S(2)}) async-start(), calls=%async_computation.2 | async-start | bytes 1310720 | tf_op jit(solution)/shard_map/psum | solution.py:118
  117.2 0.8 copy-start
  118.0 201.0 %reduce-scatter.2.cloned.1.call-start = ((), (), s32[]{:S(2)}) async-start(), calls=%async_computation.3 | async-start | bytes 4587520 | tf_op jit(solution)/shard_map/reduce_scatter | solution.py:141
Sparse Core Ops, SparseCore 0:
  24.1 83.5 all-reduce.2
  118.1 40.4 all-reduce.4
  250.9 68.0 reduce-scatter.1

commit v14 on v13

--- a/solution.py
+++ b/solution.py
@@ -62,7 +62,7 @@
                 upd = low - strict * lrow
                 return jnp.where((arow_q == k) & (acol_q >= b), lrow, upd)
 
-            low = lax.fori_loop(r0, r0 + b // STAGES, step, aug[r0:], unroll=2)
+            low = lax.fori_loop(r0, r0 + b // STAGES, step, aug[r0:], unroll=4)
             r1 = (q + 1) * b // STAGES
             parts.append(low[:r1 - r0])
             aug = jnp.concatenate(parts + ([low[r1 - r0:]] if q + 1 < STAGES else []), axis=0)

time: 326 us -> 324 us (level)
  no operation moved by 1% of the time
where the time goes in v14:
time: 324 us
  waiting for transfers between devices  192 us (59%)
  Pallas kernels  62.8 us (19%)
  matrix products  53.8 us (17%)
  between operations  13.9 us (4%)
    psum x1, waiting for transfers between devices, body(): sketch_rows = lax.psum(partial, 'rep')  83.5 us
    reduce_scatter x1, waiting for transfers between devices, body(): lax.psum_scatter(partial_sum, 'shard', scatter_dimension=0, tiled=True)  68.2 us
    pallas_call x1, Pallas kernels, chol_inverse(): pl.pallas_call(_chol_inv_kernel, out_shape=jax.ShapeDtypeStruct((n, n), j...  62.8 us
    psum x1, waiting for transfers between devices, lower_blocks_psum(): return lax.psum(packed, axis)  40.5 us
    dot_general x1, matrix products, body(): partial = jnp.dot(g, table, preferred_element_type=jnp.float32)  16.7 us
    dot_general x1, matrix products, _mm(): lax.dot_general(a, b, dims, precision=precision, preferred_element_type=j...  15.2 us
    dot_general x1, matrix products, body(): partial_sum = jnp.dot(basis_rows.T, g, preferred_element_type=jnp.float32)  12.5 us
    dot_general x1, matrix products, body(): jnp.dot(sketch_rows.T, sketch_rows, precision=lax.Precision.HIGHEST, pref...  9.34 us
  transfers between devices with their start and end apart: 3, of which 3 were waited for; matrix products, arithmetic and copies ran while one was open for 0% of the time, Pallas kernels for 0%

profile of v14, /device:TPU:0, one launch (start us, length us, event | category | flops | bytes accessed | tf_op | source)
XLA Modules:
  0.0 323.9 jit_solution(6572423863067431426)
XLA Ops:
  6.5 0.0 all-reduce.3.cloned.1.call-start
  7.2 16.7 %fusion.27 = f32[2048,512]{0,1:T(8,128)} fusion(bf16[1,2048,3584]{2,1,0:T(8,128)(2,1)} %param.2, s32[]{:T(128)} %bitcast, s32[3584]{0:T(1024)S(1)} %add_multiply_fusion), kind=kOutput, calls=%fused_computation.24 | convolution fusion | flops 7540047872 | bytes 18888708 | tf_op jit(solution)/shard_map/dot_general | solution.py:128
  23.9 0.0 all-reduce.3.cloned.1.call-update
  23.9 0.2 all-reduce.5.cloned.1.call-start
  24.2 83.5 %all-reduce.3.cloned.1.call-done = f32[2048,512]{0,1:T(8,128)} async-done(((f32[2048,512]{0,1:T(8,128)}), f32[2048,512]{0,1:T(8,128)}) %all-reduce.3.cloned.1.call-update) | async-done | bytes 4194320 | tf_op jit(solution)/shard_map/psum | solution.py:129
  107.6 9.3 %fusion.49 = f32[512,512]{1,0:T(8,128)S(1)} fusion(f32[2048,512]{0,1:T(8,128)} %all-reduce.3.cloned.1.call-done), kind=kOutput, calls=%fused_computation.54 | convolution fusion | flops 6442450944 | bytes 5242880 | tf_op jit(solution)/shard_map/dot_general | solution.py:130
  117.2 0.0 copy-start
  117.2 0.8 copy-done
  118.0 0.0 all-reduce.5.cloned.1.call-update
  118.0 0.0 reduce-scatter.2.cloned.1.call-start
  118.1 40.5 %all-reduce.5.cloned.1.call-done.g_ref = f32[10,128,128]{2,1,0:T(8,128)} async-done(((f32[10,128,128]{2,1,0:T(8,128)}), f32[10,128,128]{2,1,0:T(8,128)}) %all-reduce.5.cloned.1.call-update) | async-done | bytes 655376 | tf_op jit(solution)/shard_map/psum | solution.py:118
  158.6 62.8 %shard_map.28 = f32[512,512]{1,0:T(8,128)} custom-call(f32[10,128,128]{2,1,0:T(8,128)} %all-reduce.5.cloned.1.call-done.g_ref), custom_call_target="tpu_custom_call" | custom-call | tf_op jit(solution)/shard_map/pallas_call | solution.py:86
  221.4 15.2 %convolution_convert_fusion = bf16[2048,512]{1,0:T(8,128)(2,1)S(1)} fusion(f32[2048,512]{0,1:T(8,128)} %all-reduce.3.cloned.1.call-done, f32[512,512]{1,0:T(8,128)} %shard_map.28), kind=kOutput, calls=%fused_computation.25 | convolution fusion | flops 6443499520 | bytes 7340032 | tf_op jit(solution)/shard_map/dot_general | solution.py:15
  236.6 12.5 %fusion.13 = bf16[512,1,3584]{2,0,1:T(8,128)(2,1)} fusion(bf16[2048,512]{1,0:T(8,128)(2,1)S(1)} %convolution_convert_fusion, bf16[1,2048,3584]{2,1,0:T(8,128)(2,1)} %param.2), kind=kOutput, calls=%fused_computation.13 | convolution fusion | flops 7518027776 | bytes 20447232 | tf_op jit(solution)/shard_map/dot_general | solution.py:138
  249.1 0.0 reduce-scatter.2.cloned.1.call-update
  249.1 68.2 %reduce-scatter.2.cloned.1.call-done = bf16[128,1,3584]{2,0,1:T(8,128)(2,1)} async-done(((bf16[512,1,3584]{2,0,1:T(8,128)(2,1)}), bf16[128,1,3584]{2,0,1:T(8,128)(2,1)}) %reduce-scatter.2.cloned.1.call-update) | async-done | bytes 917520 | tf_op jit(solution)/shard_map/reduce_scatter | solution.py:141
  (11 shorter events, 0.1 us)
Async XLA Ops:
  6.5 101.1 %all-reduce.3.cloned.1.call-start = ((), (), s32[]{:S(2)}) async-start(), calls=%async_computation.1 | async-start | bytes 8388608 | tf_op jit(solution)/shard_map/psum | solution.py:129
  23.9 134.7 %all-reduce.5.cloned.1.call-start = ((), (), s32[]{:S(2)}) async-start(), calls=%async_computation.2 | async-start | bytes 1310720 | tf_op jit(solution)/shard_map/psum | solution.py:118
  117.2 0.8 copy-start
  118.0 199.4 %reduce-scatter.2.cloned.1.call-start = ((), (), s32[]{:S(2)}) async-start(), calls=%async_computation.3 | async-start | bytes 4587520 | tf_op jit(solution)/shard_map/reduce_scatter | solution.py:141
Sparse Core Ops, SparseCore 0:
  24.1 83.5 all-reduce.2
  118.1 40.4 all-reduce.4
  249.3 68.0 reduce-scatter.1
